TPU v7x, 256 devices: a whole 4x4x8 slice. The times are simulated.
256 devices in a mesh: row: 8 (over z_hi, y), col: 32 (over x, z_lo, core).
Axes of the slice: x: 4, y: 4, z: 8 (z_hi: 2, z_lo: 4; z = z_hi * 4 + z_lo), core: 2. Of those that a mesh axis runs over, the one named last changes fastest.
Arguments:
- features: bfloat16 [65536, 256], P(('row', 'col')), may hold values from -6 to 6
- weight: bfloat16 [256, 256], replicated, may hold values from -0.375 to 0.375
- cotangent: bfloat16 [65536, 256], P(('row', 'col')), may hold values from -6 to 6
- tile_values: bfloat16 [8, 8192, 128, 128], P('row', 'col'), may hold values from -0.0625 to 0.0625
- tile_rows: int32 [8, 8192], P('row', 'col'), may hold values from 0 to 63, as said below
- tile_cols: int32 [8, 8192], P('row', 'col'), may hold values from 0 to 15
- tile_count: int32 [8, 32], P('row', 'col'), may hold values from 32 to 256
Outputs:
- output: bfloat16 [65536, 256], P(('row', 'col'))
- feature_grad: bfloat16 [65536, 256], P(('row', 'col'))
- weight_grad: float32 [256, 256], replicated
Inputs may be any that keep to these rules, and one draw needn't show every extreme that they name: Within one grid block's 256 entries the pairs (tile_rows, tile_cols) are distinct; only the first tile_count entries are occupied tiles.
All inputs are finite; a program needn't handle non-finite values.
Results may differ from a plain program's by a relative error of at most 0.006.
Values may be sent and summed in bfloat16 or wider, within the bound.
No kernel may reach another device: no remote copies, remote signals or barrier semaphores. Data moves between devices by JAX's collectives and lax.ppermute only.
A program may use at most 128 MiB of HBM per device.

v0:
```python
import jax
import jax.numpy as jnp
from jax import lax
from jax.sharding import PartitionSpec as P


def group_for():
    for candidate in (64, 32, 16, 8):
        return candidate
    return 1


def tile_product(tile_block, row_ids, col_ids, occupied, source, out_rows, transpose):
    tile_side = tile_block.shape[1]
    feat_width = source.shape[1]
    group_size = group_for()
    source_tiles = source.reshape(-1, tile_side, feat_width)
    zero_rows = jnp.zeros((out_rows // tile_side, tile_side, feat_width), jnp.float32)

    def advance(group_index, summed_rows):
        first_tile = (group_index * group_size).astype(jnp.int32)
        weights = lax.dynamic_slice_in_dim(tile_block, first_tile, group_size, 0)
        row_pick = lax.dynamic_slice_in_dim(row_ids, first_tile, group_size, 0)
        col_pick = lax.dynamic_slice_in_dim(col_ids, first_tile, group_size, 0)
        in_use = first_tile + lax.iota(jnp.int32, group_size) < occupied
        if transpose:
            product = jnp.einsum(
                "kab,kaf->kbf", weights, source_tiles[row_pick], preferred_element_type=jnp.float32
            )
            target = col_pick
        else:
            product = jnp.einsum(
                "kab,kbf->kaf", weights, source_tiles[col_pick], preferred_element_type=jnp.float32
            )
            target = row_pick
        product = jnp.where(in_use[:, None, None], product, jnp.zeros_like(product))
        return summed_rows.at[target].add(product)

    turn_count = (occupied + group_size - 1) // group_size
    summed_rows = lax.fori_loop(jnp.int32(0), turn_count, advance, zero_rows)
    return summed_rows.reshape(out_rows, feat_width)


def silu_grad(cot_part, pre_part):
    sigma = jax.nn.sigmoid(pre_part)
    return (cot_part.astype(jnp.float32) * (sigma * (1.0 + pre_part * (1.0 - sigma)))).astype(
        jnp.bfloat16
    )


def per_device(features, weight, cotangent, tile_values, tile_rows, tile_cols, tile_count):
    node_rows = features.shape[0]
    row_devices = lax.axis_size("row")
    col_devices = lax.axis_size("col")
    tile_block = tile_values[0]
    row_ids = tile_rows[0]
    col_ids = tile_cols[0]
    occupied = tile_count[0, 0]
    projected = jnp.dot(features, weight, preferred_element_type=jnp.float32).astype(jnp.bfloat16)
    column_source = lax.all_gather(projected, "row", axis=0, tiled=True)
    partial_value = tile_product(
        tile_block, row_ids, col_ids, occupied, column_source, col_devices * node_rows, False
    )
    pre = lax.psum_scatter(partial_value, "col", scatter_dimension=0, tiled=True)
    grad_pre = silu_grad(cotangent, pre)
    row_source = lax.all_gather(grad_pre, "col", axis=0, tiled=True)
    output = jax.nn.silu(pre).astype(jnp.bfloat16)
    back_terms = tile_product(
        tile_block, row_ids, col_ids, occupied, row_source, row_devices * node_rows, True
    )
    aggregated = lax.psum_scatter(back_terms, "row", scatter_dimension=0, tiled=True)
    node_grad = aggregated.astype(jnp.bfloat16)
    feature_grad = jnp.dot(node_grad, weight.T, preferred_element_type=jnp.float32).astype(
        jnp.bfloat16
    )
    local_term = jnp.dot(features.T, node_grad, preferred_element_type=jnp.float32)
    grad_scale = float(node_rows * row_devices * col_devices) ** (-0.5)
    weight_grad = lax.psum(local_term, ("row", "col")) * grad_scale
    return (output, feature_grad, weight_grad)


def solution(mesh):
    placed = (
        P(("row", "col"), None),
        P(),
        P(("row", "col"), None),
        P("row", "col", None, None),
        P("row", "col"),
        P("row", "col"),
        P("row", "col"),
    )
    return jax.shard_map(
        per_device,
        mesh=mesh,
        in_specs=placed,
        out_specs=(P(("row", "col"), None), P(("row", "col"), None), P()),
        check_vma=False,
    )
```

profile of v0, /device:TPU:4, one launch (start us, length us, event | category | flops | bytes accessed | tf_op | source)
XLA Modules:
  0.0 882.0 jit_solution(2255266839701614296)
XLA Ops:
  7.2 0.0 all-gather.3.cloned.1.call-start
  7.2 0.8 copy-done
  8.1 1.7 convolution_convert_fusion.1
  9.8 0.0 all-gather.3.cloned.1.call-update
  9.8 0.0 reduce-scatter.3.cloned.1.call-start
  10.6 65.3 %all-gather.3.cloned.1.call-done = bf16[2048,256]{1,0:T(8,128)(2,1)} async-done(((bf16[256,256]{1,0:T(8,128)(2,1)}), bf16[2048,256]{1,0:T(8,128)(2,1)}) %all-gather.3.cloned.1.call-update) | async-done | bytes 1048592 | tf_op jit(solution)/shard_map/all_gather | solution.py:60
  75.9 4.3 broadcast.47
  80.2 60.9 %while.20 = (s32[]{:T(128)}, f32[64,128,256]{2,1,0:T(8,128)}, s32[]{:T(128)}, s32[256]{0:T(256)S(1)}, s32[]{:T(128)}, /*index=5*/bf16[256,128,128]{2,1,0:T(8,128...) while((s32[]{:T(128)}, f32[64,128,256]{2,1,0:T(8,128)}, ...), condition=%wide.region_2.3_spmd, body=%wide.region_0.2_spmd.sunk | while | flops 541066752 | bytes 48240696 | solution.py:40
  80.2 0.1 compare_select_fusion.6
  80.3 0.7 add_compare_fusion.4
  80.9 2.8 gather_fusion
  83.7 7.3 broadcast_select_fusion.4
  91.0 19.7 %scatter_fusion = f32[64,128,256]{2,1,0:T(8,128)} fusion(f32[64,128,256]{2,1,0:T(8,128)} %get-tuple-element.261, s32[64]{0:T(128)S(1)} %get-tuple-element.236, f32[64,128,256]{2,1,0:T(8,128)} %broadcast_select_fusion.4), kind=kCustom, calls=%fused_computation.2.clone.1 | custom fusion | flops 2097152 | bytes 25166080 | tf_op jit(solution)/shard_map/while/body/scatter-add | solution.py:37
  110.7 0.1 compare_select_fusion.6
  110.8 0.7 add_compare_fusion.4
  111.5 2.8 gather_fusion
  114.2 7.3 broadcast_select_fusion.4
  121.5 19.6 %scatter_fusion = f32[64,128,256]{2,1,0:T(8,128)} fusion(f32[64,128,256]{2,1,0:T(8,128)} %get-tuple-element.261, s32[64]{0:T(128)S(1)} %get-tuple-element.236, f32[64,128,256]{2,1,0:T(8,128)} %broadcast_select_fusion.4), kind=kCustom, calls=%fused_computation.2.clone.1 | custom fusion | flops 2097152 | bytes 25166080 | tf_op jit(solution)/shard_map/while/body/scatter-add | solution.py:37
  141.1 0.0 reduce-scatter.3.cloned.1.call-update
  141.1 0.0 all-gather.5.cloned.1.call-start
  141.2 199.5 %reduce-scatter.3.cloned.1.call-done = f32[256,256]{1,0:T(8,128)} async-done(((f32[8192,256]{1,0:T(8,128)}), f32[256,256]{1,0:T(8,128)}) %reduce-scatter.3.cloned.1.call-update) | async-done | bytes 262160 | tf_op jit(solution)/shard_map/reduce_scatter | solution.py:64
  340.7 1.8 multiply_convert_fusion
  342.4 0.0 all-gather.5.cloned.1.call-update
  342.4 0.0 reduce-scatter.5.cloned.1.call-start
  342.5 12.0 %copy.10 = bf16[1,256,128,128]{2,3,1,0:T(8,128)(2,1)} copy(bf16[1,256,128,128]{3,2,1,0:T(8,128)(2,1)} %bitcast.27) | data formatting | bytes 16777216 | tf_op args[3]
  354.5 66.2 %all-gather.5.cloned.1.call-done = bf16[8192,256]{1,0:T(8,128)(2,1)} async-done(((bf16[256,256]{1,0:T(8,128)(2,1)}), bf16[8192,256]{1,0:T(8,128)(2,1)}) %all-gather.5.cloned.1.call-update) | async-done | bytes 4194320 | tf_op jit(solution)/shard_map/all_gather | solution.py:66
  420.7 0.2 broadcast_in_dim.30
  421.0 50.9 %while.21 = (s32[]{:T(128)}, f32[16,128,256]{2,1,0:T(8,128)S(1)}, s32[]{:T(128)}, s32[256]{0:T(256)S(1)}, s32[]{:T(128)}, /*index=5*/bf16[256,128,128]{1,2,0:T(8...) while((s32[]{:T(128)}, f32[16,128,256]{2,1,0:T(8,128)S(1)}, ...), condition=%wide.region_6.7_spmd, body=%wide.region_4.6_spmd.sunk | while | flops 541066752 | bytes 48240696 | solution.py:40
  421.0 0.1 compare_select_fusion.7
  421.1 0.7 add_compare_fusion.5
  421.7 5.0 gather_fusion.1
  426.7 7.3 broadcast_select_fusion.5
  434.0 12.4 %scatter_fusion.1 = f32[16,128,256]{2,1,0:T(8,128)S(1)} fusion(f32[16,128,256]{2,1,0:T(8,128)S(1)} %get-tuple-element.297, s32[64]{0:T(128)S(1)} %get-tuple-element.246, f32[64,128,256]{2,1,0:T(8,128)} %broadcast_select_fusion.5), kind=kCustom, calls=%fused_computation.3.clone.1 | custom fusion | flops 2097152 | bytes 25166080 | tf_op jit(solution)/shard_map/while/body/scatter-add | solution.py:37
  446.5 0.1 compare_select_fusion.7
  446.5 0.7 add_compare_fusion.5
  447.2 5.0 gather_fusion.1
  452.2 7.3 broadcast_select_fusion.5
  459.5 12.4 %scatter_fusion.1 = f32[16,128,256]{2,1,0:T(8,128)S(1)} fusion(f32[16,128,256]{2,1,0:T(8,128)S(1)} %get-tuple-element.297, s32[64]{0:T(128)S(1)} %get-tuple-element.246, f32[64,128,256]{2,1,0:T(8,128)} %broadcast_select_fusion.5), kind=kCustom, calls=%fused_computation.3.clone.1 | custom fusion | flops 2097152 | bytes 25166080 | tf_op jit(solution)/shard_map/while/body/scatter-add | solution.py:37
  471.9 1.3 copy-done.1
  473.2 0.0 reduce-scatter.5.cloned.1.call-update
  473.3 0.0 all-reduce.2.cloned.1.call-start
  473.3 144.3 %reduce-scatter.5.cloned.1.call-done = f32[256,256]{1,0:T(8,128)} async-done(((f32[2048,256]{1,0:T(8,128)}), f32[256,256]{1,0:T(8,128)}) %reduce-scatter.5.cloned.1.call-update) | async-done | bytes 262160 | tf_op jit(solution)/shard_map/reduce_scatter | solution.py:71
  617.6 1.9 convolution_bitcast_fusion
  619.5 0.0 all-reduce.2.cloned.1.call-update
  619.6 1.8 convolution_convert_fusion
  621.4 252.3 %all-reduce.2.cloned.1.call-done = f32[256,256]{0,1:T(8,128)} async-done(((f32[256,256]{0,1:T(8,128)}), f32[256,256]{0,1:T(8,128)}) %all-reduce.2.cloned.1.call-update) | async-done | bytes 262160 | tf_op jit(solution)/shard_map/psum | solution.py:78
  873.7 1.0 broadcast_multiply_fusion
  874.6 0.8 copy.12
  (16 shorter events, 0.1 us)
Async XLA Ops:
  7.2 0.9 copy-start
  7.2 68.7 %all-gather.3.cloned.1.call-start = ((), (), s32[]{:S(2)}) async-start(), calls=%async_computation.2 | async-start | bytes 1179648 | tf_op jit(solution)/shard_map/all_gather | solution.py:60
  9.8 330.8 %reduce-scatter.3.cloned.1.call-start = ((), (), s32[]{:S(2)}) async-start(), calls=%async_computation.3 | async-start | bytes 8650752 | tf_op jit(solution)/shard_map/reduce_scatter | solution.py:64
  75.9 4.3 copy-start.2
  75.9 4.3 copy-start.5
  75.9 4.3 copy-start.6
  141.1 199.5 %copy-start.4 = (bf16[256,256]{1,0:T(8,128)(2,1)S(1)}, bf16[256,256]{1,0:T(8,128)(2,1)}, u32[]{:S(2)}) copy-start(bf16[256,256]{1,0:T(8,128)(2,1)} %param.13) | copy-start | bytes 393220
  141.1 279.6 %all-gather.5.cloned.1.call-start = ((), (), s32[]{:S(2)}) async-start(), calls=%async_computation.4 | async-start | bytes 4325376 | tf_op jit(solution)/shard_map/all_gather | solution.py:66
  342.4 275.2 %reduce-scatter.5.cloned.1.call-start = ((), (), s32[]{:S(2)}) async-start(), calls=%async_computation.5 | async-start | bytes 2359296 | tf_op jit(solution)/shard_map/reduce_scatter | solution.py:71
  420.9 198.6 %copy-start.3 = (bf16[256,256]{1,0:T(8,128)(2,1)S(1)}, bf16[256,256]{1,0:T(8,128)(2,1)}, u32[]{:S(2)}) copy-start(bf16[256,256]{1,0:T(8,128)(2,1)} %param.12) | copy-start | bytes 393220
  471.9 1.3 copy-start.1
  473.3 400.4 %all-reduce.2.cloned.1.call-start = ((), (), s32[]{:S(2)}) async-start(), calls=%async_computation.6 | async-start | bytes 524288 | tf_op jit(solution)/shard_map/psum | solution.py:78
Sparse Core Ops, SparseCore 0:
  11.2 64.6 all-gather.2
  141.3 199.3 reduce-scatter.2
  343.1 77.6 all-gather.4
  473.4 144.2 reduce-scatter.4
  623.5 250.0 all-reduce.1
where the time goes:
time: 883 us; the launch traced here: 882 us
  waiting for transfers between devices  728 us (82%)
  other arithmetic  69.9 us (8%)
  local copies, waits for them, and re-layouts  35 us (4%)
  matrix products  34.6 us (4%)
  between operations  14.5 us (2%)
    psum x1, waiting for transfers between devices, per_device(): weight_grad = lax.psum(local_term, ('row', 'col')) * grad_scale  252 us
    reduce_scatter x1, waiting for transfers between devices, per_device(): lax.psum_scatter(partial_value, 'col', scatter_dimension=0, tiled=True)  199 us
    reduce_scatter x1, waiting for transfers between devices, per_device(): lax.psum_scatter(back_terms, 'row', scatter_dimension=0, tiled=True)  144 us
    all_gather x1, waiting for transfers between devices, per_device(): row_source = lax.all_gather(grad_pre, 'col', axis=0, tiled=True)  66.2 us
    all_gather x1, waiting for transfers between devices, per_device(): column_source = lax.all_gather(projected, 'row', axis=0, tiled=True)  65.3 us
    scatter-add x4, other arithmetic, advance(): return summed_rows.at[target].add(product)  64.2 us
  transfers between devices with their start and end apart: 5, of which 5 were waited for; matrix products, arithmetic and copies ran while one was open for 2% of the time, Pallas kernels for 0%

commit v1 on v0

--- a/solution.py
+++ b/solution.py
@@ -1,44 +1,77 @@
 import jax
 import jax.numpy as jnp
 from jax import lax
+from jax.experimental import pallas as pl
+from jax.experimental.pallas import tpu as pltpu
 from jax.sharding import PartitionSpec as P
 
-
-def group_for():
-    for candidate in (64, 32, 16, 8):
-        return candidate
-    return 1
+GROUP = 16
 
 
 def tile_product(tile_block, row_ids, col_ids, occupied, source, out_rows, transpose):
-    tile_side = tile_block.shape[1]
+    tile_count, tile_side, _ = tile_block.shape
     feat_width = source.shape[1]
-    group_size = group_for()
-    source_tiles = source.reshape(-1, tile_side, feat_width)
-    zero_rows = jnp.zeros((out_rows // tile_side, tile_side, feat_width), jnp.float32)
+    src_rows = source.shape[0]
+    row_limit = (src_rows if transpose else out_rows) // tile_side - 1
+    col_limit = (out_rows if transpose else src_rows) // tile_side - 1
+    steps = tile_count // GROUP
 
-    def advance(group_index, summed_rows):
-        first_tile = (group_index * group_size).astype(jnp.int32)
-        weights = lax.dynamic_slice_in_dim(tile_block, first_tile, group_size, 0)
-        row_pick = lax.dynamic_slice_in_dim(row_ids, first_tile, group_size, 0)
-        col_pick = lax.dynamic_slice_in_dim(col_ids, first_tile, group_size, 0)
-        in_use = first_tile + lax.iota(jnp.int32, group_size) < occupied
-        if transpose:
-            product = jnp.einsum(
-                "kab,kaf->kbf", weights, source_tiles[row_pick], preferred_element_type=jnp.float32
-            )
-            target = col_pick
-        else:
-            product = jnp.einsum(
-                "kab,kbf->kaf", weights, source_tiles[col_pick], preferred_element_type=jnp.float32
-            )
-            target = row_pick
-        product = jnp.where(in_use[:, None, None], product, jnp.zeros_like(product))
-        return summed_rows.at[target].add(product)
+    def kernel(rows_ref, cols_ref, cnt_ref, tiles_ref, src_ref, out_ref):
+        g = pl.program_id(0)
+        cnt = cnt_ref[0]
 
-    turn_count = (occupied + group_size - 1) // group_size
-    summed_rows = lax.fori_loop(jnp.int32(0), turn_count, advance, zero_rows)
-    return summed_rows.reshape(out_rows, feat_width)
+        @pl.when(g == 0)
+        def _():
+            out_ref[...] = jnp.zeros_like(out_ref)
+
+        @pl.when(g * GROUP < cnt)
+        def _():
+            def body(t, carry):
+                k = g * GROUP + t
+
+                @pl.when(k < cnt)
+                def _():
+                    r = jnp.clip(rows_ref[k], 0, row_limit)
+                    c = jnp.clip(cols_ref[k], 0, col_limit)
+                    a = tiles_ref[t]
+                    if transpose:
+                        s = src_ref[pl.ds(pl.multiple_of(r * tile_side, tile_side), tile_side), :]
+                        prod = lax.dot_general(
+                            a, s, (((0,), (0,)), ((), ())), preferred_element_type=jnp.float32
+                        )
+                        dst = c
+                    else:
+                        s = src_ref[pl.ds(pl.multiple_of(c * tile_side, tile_side), tile_side), :]
+                        prod = jnp.dot(a, s, preferred_element_type=jnp.float32)
+                        dst = r
+                    sl = pl.ds(pl.multiple_of(dst * tile_side, tile_side), tile_side)
+                    out_ref[sl, :] += prod
+
+                return carry
+
+            lax.fori_loop(0, GROUP, body, 0, unroll=True)
+
+    def tile_map(g, rows_ref, cols_ref, cnt_ref):
+        last = jnp.maximum(cnt_ref[0] - 1, 0) // GROUP
+        return (jnp.minimum(g, last), 0, 0)
+
+    grid_spec = pltpu.PrefetchScalarGridSpec(
+        num_scalar_prefetch=3,
+        grid=(steps,),
+        in_specs=[
+            pl.BlockSpec((GROUP, tile_side, tile_side), tile_map),
+            pl.BlockSpec((src_rows, feat_width), lambda g, *_: (0, 0)),
+        ],
+        out_specs=pl.BlockSpec((out_rows, feat_width), lambda g, *_: (0, 0)),
+    )
+    return pl.pallas_call(
+        kernel,
+        grid_spec=grid_spec,
+        out_shape=jax.ShapeDtypeStruct((out_rows, feat_width), jnp.float32),
+        compiler_params=pltpu.CompilerParams(
+            dimension_semantics=("arbitrary",), vmem_limit_bytes=48 * 1024 * 1024
+        ),
+    )(row_ids, col_ids, occupied.reshape(1), tile_block, source)
 
 
 def silu_grad(cot_part, pre_part):

time: 883 us -> 752 us (0.85)
  waiting for transfers between devices: 728 us -> 651 us
  Pallas kernels: 0 us -> 72.5 us
  other arithmetic: 69.9 us -> 2.74 us
  local copies, waits for them, and re-layouts: 35 us -> 4.29 us
  matrix products: 34.6 us -> 5.46 us
    pallas_call x0 -> x2, Pallas kernels: none -> 72.5 us  [tile_product(): pl.pallas_call(kernel, grid_spec=grid_spec, out_shape=jax.ShapeDtypeStruc...]
    scatter-add x4 -> x0, other arithmetic: 64.2 us -> none  [advance(): return summed_rows.at[target].add(product)]
    reduce_scatter x1, waiting for transfers between devices: 199 us -> 148 us  [per_device(): lax.psum_scatter(partial_value, 'col', scatter_dimension=0, tiled=True)]
    reduce_scatter x1, waiting for transfers between devices: 144 us -> 107 us  [per_device(): lax.psum_scatter(back_terms, 'row', scatter_dimension=0, tiled=True)]
    dot_general x4 -> x0, matrix products: 29.1 us -> none  [the longest x2 14.6 us: advance(): jnp.einsum('kab,kaf->kbf', weights, source_tiles[row_pick], preferred_ele...]
    gather x4 -> x0, local copies, waits for them, and re-layouts: 15.4 us -> none  [the longest x2 9.93 us: advance(): source_tiles[row_pick]]
    all_gather x1, waiting for transfers between devices: 66.2 us -> 78.2 us  [per_device(): row_source = lax.all_gather(grad_pre, 'col', axis=0, tiled=True)]
    unnamed x16 -> x17, local copies, waits for them, and re-layouts: 15 us -> 4.29 us
  transfers between devices with their start and end apart: 5 -> 5, of which waited for: 5 -> 5; matrix products, arithmetic and copies ran while one was open for 2% -> 0% of each run, Pallas kernels for 0% -> 0%
where the time goes in v1:
time: 752 us; the launch traced here: 751 us
  waiting for transfers between devices  651 us (87%)
  Pallas kernels  72.5 us (10%)
  between operations  14.5 us (2%)
    psum x1, waiting for transfers between devices, per_device(): weight_grad = lax.psum(local_term, ('row', 'col')) * grad_scale  252 us
    reduce_scatter x1, waiting for transfers between devices, per_device(): lax.psum_scatter(partial_value, 'col', scatter_dimension=0, tiled=True)  148 us
    reduce_scatter x1, waiting for transfers between devices, per_device(): lax.psum_scatter(back_terms, 'row', scatter_dimension=0, tiled=True)  107 us
    all_gather x1, waiting for transfers between devices, per_device(): row_source = lax.all_gather(grad_pre, 'col', axis=0, tiled=True)  78.2 us
    pallas_call x2, Pallas kernels, tile_product(): pl.pallas_call(kernel, grid_spec=grid_spec, out_shape=jax.ShapeDtypeStruc...  72.5 us
    all_gather x1, waiting for transfers between devices, per_device(): column_source = lax.all_gather(projected, 'row', axis=0, tiled=True)  65.4 us
  transfers between devices with their start and end apart: 5, of which 5 were waited for; matrix products, arithmetic and copies ran while one was open for 0% of the time, Pallas kernels for 0%

profile of v1, /device:TPU:4, one launch (start us, length us, event | category | flops | bytes accessed | tf_op | source)
XLA Modules:
  0.0 750.6 jit_solution(9964485478931437024)
XLA Ops:
  7.2 0.0 copy-start
  7.2 0.0 all-gather.3.cloned.1.call-start
  7.2 0.8 copy-done
  8.1 1.7 convolution_convert_fusion.1
  9.8 0.0 all-gather.3.cloned.1.call-update
  9.8 0.0 reduce-scatter.3.cloned.1.call-start
  10.5 65.4 %all-gather.3.cloned.1.call-done.src_ref = bf16[2048,256]{1,0:T(8,128)(2,1)} async-done(((bf16[256,256]{1,0:T(8,128)(2,1)}), bf16[2048,256]{1,0:T(8,128)(2,1)}) %all-gather.3.cloned.1.call-update) | async-done | bytes 1048592 | tf_op jit(solution)/shard_map/all_gather | solution.py:93
  75.9 0.0 copy-start.1
  75.9 1.2 copy-done.1
  77.1 0.0 copy-start.2
  77.1 0.7 copy-done.2
  77.8 0.0 copy-start.4
  77.8 0.7 copy-done.4
  78.5 32.7 %shard_map.94 = f32[8192,256]{1,0:T(8,128)} custom-call(s32[256]{0:T(256)S(1)} %bitcast.12, s32[256]{0:T(256)S(1)} %bitcast.14, s32[1]{0:T(128)} %bitcast.10.cnt_ref, bf16[256,128,128]{2,1,0:T(8,128)(2,1)} %bitcast.16, bf16[2048,256]{1,0:T(8,128)(2,1)S(1)} %copy-done.1), custom_call_target="tpu_custom_call" | custom-call | tf_op jit(solution)/shard_map/pallas_call | solution.py:67
  111.2 0.0 copy-start.7
  111.2 0.0 copy-start.3
  111.2 0.0 copy-start.5
  111.2 0.0 reduce-scatter.3.cloned.1.call-update
  111.2 0.0 all-gather.5.cloned.1.call-start
  111.3 147.8 %reduce-scatter.3.cloned.1.call-done = f32[256,256]{1,0:T(8,128)} async-done(((f32[8192,256]{1,0:T(8,128)}), f32[256,256]{1,0:T(8,128)}) %reduce-scatter.3.cloned.1.call-update) | async-done | bytes 262160 | tf_op jit(solution)/shard_map/reduce_scatter | solution.py:97
  259.0 0.0 copy-done.7
  259.0 1.8 multiply_convert_fusion
  260.8 0.0 all-gather.5.cloned.1.call-update
  260.8 0.0 reduce-scatter.5.cloned.1.call-start
  260.9 78.2 %all-gather.5.cloned.1.call-done.src_ref = bf16[8192,256]{1,0:T(8,128)(2,1)} async-done(((bf16[256,256]{1,0:T(8,128)(2,1)}), bf16[8192,256]{1,0:T(8,128)(2,1)}) %all-gather.5.cloned.1.call-update) | async-done | bytes 4194320 | tf_op jit(solution)/shard_map/all_gather | solution.py:99
  339.1 0.0 copy-done.3
  339.1 0.0 copy-done.5
  339.1 0.0 copy-start.6
  339.1 39.8 %shard_map.95 = f32[2048,256]{1,0:T(8,128)} custom-call(s32[256]{0:T(256)S(1)} %bitcast.13, s32[256]{0:T(256)S(1)} %bitcast.15, s32[1]{0:T(128)} %bitcast.11.cnt_ref, bf16[256,128,128]{2,1,0:T(8,128)(2,1)} %bitcast.17, bf16[8192,256]{1,0:T(8,128)(2,1)} %all-gather.5.cloned.1.call-done.src_ref), custom_call_target="tpu_custom_call" | custom-call | tf_op jit(solution)/shard_map/pallas_call | solution.py:67
  378.9 0.0 reduce-scatter.5.cloned.1.call-update
  378.9 0.0 all-reduce.2.cloned.1.call-start
  379.0 107.1 %reduce-scatter.5.cloned.1.call-done = f32[256,256]{1,0:T(8,128)} async-done(((f32[2048,256]{1,0:T(8,128)}), f32[256,256]{1,0:T(8,128)}) %reduce-scatter.5.cloned.1.call-update) | async-done | bytes 262160 | tf_op jit(solution)/shard_map/reduce_scatter | solution.py:104
  486.1 1.9 convolution_bitcast_fusion
  488.0 0.0 all-reduce.2.cloned.1.call-update
  488.0 0.0 copy-done.6
  488.0 1.8 convolution_convert_fusion
  489.8 252.4 %all-reduce.2.cloned.1.call-done = f32[256,256]{0,1:T(8,128)} async-done(((f32[256,256]{0,1:T(8,128)}), f32[256,256]{0,1:T(8,128)}) %all-reduce.2.cloned.1.call-update) | async-done | bytes 262160 | tf_op jit(solution)/shard_map/psum | solution.py:111
  742.2 1.0 broadcast_multiply_fusion
  743.2 0.8 copy.10
Async XLA Ops:
  7.2 0.9 copy-start
  7.2 68.7 %all-gather.3.cloned.1.call-start = ((), (), s32[]{:S(2)}) async-start(), calls=%async_computation.2 | async-start | bytes 1179648 | tf_op jit(solution)/shard_map/all_gather | solution.py:93
  9.8 249.2 %reduce-scatter.3.cloned.1.call-start = ((), (), s32[]{:S(2)}) async-start(), calls=%async_computation.3 | async-start | bytes 8650752 | tf_op jit(solution)/shard_map/reduce_scatter | solution.py:97
  75.9 1.2 copy-start.1
  77.1 0.7 copy-start.2
  77.8 0.7 copy-start.4
  111.2 147.8 %copy-start.7 = (bf16[256,256]{1,0:T(8,128)(2,1)S(1)}, bf16[256,256]{1,0:T(8,128)(2,1)}, u32[]{:S(2)}) copy-start(bf16[256,256]{1,0:T(8,128)(2,1)} %param.9) | copy-start | bytes 393220
  111.2 227.9 %copy-start.3 = (s32[1,256]{1,0:T(1,128)S(1)}, s32[1,256]{1,0:T(1,128)}, u32[]{:S(2)}) copy-start(s32[1,256]{1,0:T(1,128)} %param.11) | copy-start | bytes 3076
  111.2 227.9 %copy-start.5 = (s32[1,256]{1,0:T(1,128)S(1)}, s32[1,256]{1,0:T(1,128)}, u32[]{:S(2)}) copy-start(s32[1,256]{1,0:T(1,128)} %param.12) | copy-start | bytes 3076
  111.2 227.9 %all-gather.5.cloned.1.call-start = ((), (), s32[]{:S(2)}) async-start(), calls=%async_computation.4 | async-start | bytes 4325376 | tf_op jit(solution)/shard_map/all_gather | solution.py:99
  260.8 225.3 %reduce-scatter.5.cloned.1.call-start = ((), (), s32[]{:S(2)}) async-start(), calls=%async_computation.5 | async-start | bytes 2359296 | tf_op jit(solution)/shard_map/reduce_scatter | solution.py:104
  339.1 148.9 %copy-start.6 = (bf16[256,256]{1,0:T(8,128)(2,1)S(1)}, bf16[256,256]{1,0:T(8,128)(2,1)}, u32[]{:S(2)}) copy-start(bf16[256,256]{1,0:T(8,128)(2,1)} %param.8) | copy-start | bytes 393220
  378.9 363.3 %all-reduce.2.cloned.1.call-start = ((), (), s32[]{:S(2)}) async-start(), calls=%async_computation.6 | async-start | bytes 524288 | tf_op jit(solution)/shard_map/psum | solution.py:111
Sparse Core Ops, SparseCore 0:
  11.2 64.6 all-gather.2
  111.3 147.6 reduce-scatter.2
  261.5 77.5 all-gather.4
  379.1 106.9 reduce-scatter.4
  492.0 250.2 all-reduce.1

commit v2 on v1

--- a/solution.py
+++ b/solution.py
@@ -8,7 +8,7 @@
 GROUP = 16
 
 
-def tile_product(tile_block, row_ids, col_ids, occupied, source, out_rows, transpose):
+def tile_product(tile_block, row_ids, col_ids, occupied, source, out_rows, transpose, out_dtype):
     tile_count, tile_side, _ = tile_block.shape
     feat_width = source.shape[1]
     src_rows = source.shape[0]
@@ -16,13 +16,13 @@
     col_limit = (out_rows if transpose else src_rows) // tile_side - 1
     steps = tile_count // GROUP
 
-    def kernel(rows_ref, cols_ref, cnt_ref, tiles_ref, src_ref, out_ref):
+    def kernel(rows_ref, cols_ref, cnt_ref, tiles_ref, src_ref, out_ref, acc_ref):
         g = pl.program_id(0)
         cnt = cnt_ref[0]
 
         @pl.when(g == 0)
         def _():
-            out_ref[...] = jnp.zeros_like(out_ref)
+            acc_ref[...] = jnp.zeros_like(acc_ref)
 
         @pl.when(g * GROUP < cnt)
         def _():
@@ -45,11 +45,15 @@
                         prod = jnp.dot(a, s, preferred_element_type=jnp.float32)
                         dst = r
                     sl = pl.ds(pl.multiple_of(dst * tile_side, tile_side), tile_side)
-                    out_ref[sl, :] += prod
+                    acc_ref[sl, :] += prod
 
                 return carry
 
             lax.fori_loop(0, GROUP, body, 0, unroll=True)
+
+        @pl.when(g == steps - 1)
+        def _():
+            out_ref[...] = acc_ref[...].astype(out_ref.dtype)
 
     def tile_map(g, rows_ref, cols_ref, cnt_ref):
         last = jnp.maximum(cnt_ref[0] - 1, 0) // GROUP
@@ -63,15 +67,33 @@
             pl.BlockSpec((src_rows, feat_width), lambda g, *_: (0, 0)),
         ],
         out_specs=pl.BlockSpec((out_rows, feat_width), lambda g, *_: (0, 0)),
+        scratch_shapes=[pltpu.VMEM((out_rows, feat_width), jnp.float32)],
     )
     return pl.pallas_call(
         kernel,
         grid_spec=grid_spec,
-        out_shape=jax.ShapeDtypeStruct((out_rows, feat_width), jnp.float32),
+        out_shape=jax.ShapeDtypeStruct((out_rows, feat_width), out_dtype),
         compiler_params=pltpu.CompilerParams(
             dimension_semantics=("arbitrary",), vmem_limit_bytes=48 * 1024 * 1024
         ),
     )(row_ids, col_ids, occupied.reshape(1), tile_block, source)
+
+
+def reduce_blocks(partial_value, axis, devices):
+    pieces = partial_value.reshape(devices, -1, partial_value.shape[1])
+    received = lax.all_to_all(pieces, axis, 0, 0, tiled=False)
+    return received.astype(jnp.float32).sum(0)
+
+
+def butterfly_sum(value, axes):
+    for axis in axes:
+        size = lax.axis_size(axis)
+        step = 1
+        while step < size:
+            pairs = [(i, i ^ step) for i in range(size)]
+            value = value + lax.ppermute(value, axis, pairs)
+            step *= 2
+    return value
 
 
 def silu_grad(cot_part, pre_part):
@@ -92,23 +114,25 @@
     projected = jnp.dot(features, weight, preferred_element_type=jnp.float32).astype(jnp.bfloat16)
     column_source = lax.all_gather(projected, "row", axis=0, tiled=True)
     partial_value = tile_product(
-        tile_block, row_ids, col_ids, occupied, column_source, col_devices * node_rows, False
+        tile_block, row_ids, col_ids, occupied, column_source, col_devices * node_rows, False,
+        jnp.bfloat16,
     )
-    pre = lax.psum_scatter(partial_value, "col", scatter_dimension=0, tiled=True)
+    pre = reduce_blocks(partial_value, "col", col_devices)
     grad_pre = silu_grad(cotangent, pre)
     row_source = lax.all_gather(grad_pre, "col", axis=0, tiled=True)
     output = jax.nn.silu(pre).astype(jnp.bfloat16)
     back_terms = tile_product(
-        tile_block, row_ids, col_ids, occupied, row_source, row_devices * node_rows, True
+        tile_block, row_ids, col_ids, occupied, row_source, row_devices * node_rows, True,
+        jnp.bfloat16,
     )
-    aggregated = lax.psum_scatter(back_terms, "row", scatter_dimension=0, tiled=True)
+    aggregated = reduce_blocks(back_terms, "row", row_devices)
     node_grad = aggregated.astype(jnp.bfloat16)
     feature_grad = jnp.dot(node_grad, weight.T, preferred_element_type=jnp.float32).astype(
         jnp.bfloat16
     )
     local_term = jnp.dot(features.T, node_grad, preferred_element_type=jnp.float32)
     grad_scale = float(node_rows * row_devices * col_devices) ** (-0.5)
-    weight_grad = lax.psum(local_term, ("row", "col")) * grad_scale
+    weight_grad = butterfly_sum(local_term, ("col", "row")) * grad_scale
     return (output, feature_grad, weight_grad)
 
 

time: 752 us -> 430 us (0.57)
  waiting for transfers between devices: 651 us -> 189 us
  blocking collectives: 0 us -> 123 us
  starting transfers between devices: 0.21 us -> 24.2 us
    reduce_scatter x2 -> x0, waiting for transfers between devices: 255 us -> none  [the longest x1 148 us: per_device(): lax.psum_scatter(partial_value, 'col', scatter_dimension=0, tiled=True)]
    psum x1 -> x0, waiting for transfers between devices: 252 us -> none  [per_device(): weight_grad = lax.psum(local_term, ('row', 'col')) * grad_scale]
    all_to_all x0 -> x2, blocking collectives: none -> 123 us  [reduce_blocks(): received = lax.all_to_all(pieces, axis, 0, 0, tiled=False)]
    ppermute x0 -> x8, waiting for transfers between devices: none -> 58.1 us  [butterfly_sum(): value = value + lax.ppermute(value, axis, pairs)]
    ppermute x0 -> x8, starting transfers between devices: none -> 24.2 us  [butterfly_sum(): value = value + lax.ppermute(value, axis, pairs)]
    all_gather x1, waiting for transfers between devices: 78.2 us -> 65.2 us  [per_device(): row_source = lax.all_gather(grad_pre, 'col', axis=0, tiled=True)]
  transfers between devices with their start and end apart: 5 -> 10, of which waited for: 5 -> 10; matrix products, arithmetic and copies ran while one was open for 0% -> 0% of each run, Pallas kernels for 0% -> 0%
where the time goes in v2:
time: 430 us; the launch traced here: 429 us
  waiting for transfers between devices  189 us (44%)
  blocking collectives  123 us (29%)
  Pallas kernels  67.2 us (16%)
  starting transfers between devices  24.2 us (6%)
  between operations  14.8 us (3%)
  local copies, waits for them, and re-layouts  6.79 us (2%)
    all_to_all x2, blocking collectives, reduce_blocks(): received = lax.all_to_all(pieces, axis, 0, 0, tiled=False)  123 us
    pallas_call x2, Pallas kernels, tile_product(): pl.pallas_call(kernel, grid_spec=grid_spec, out_shape=jax.ShapeDtypeStruc...  67.2 us
    all_gather x1, waiting for transfers between devices, per_device(): column_source = lax.all_gather(projected, 'row', axis=0, tiled=True)  65.4 us
    all_gather x1, waiting for transfers between devices, per_device(): row_source = lax.all_gather(grad_pre, 'col', axis=0, tiled=True)  65.2 us
    ppermute x8, waiting for transfers between devices, butterfly_sum(): value = value + lax.ppermute(value, axis, pairs)  58.1 us
    ppermute x8, starting transfers between devices, butterfly_sum(): value = value + lax.ppermute(value, axis, pairs)  24.2 us
  transfers between devices with their start and end apart: 10, of which 10 were waited for; matrix products, arithmetic and copies ran while one was open for 0% of the time, Pallas kernels for 0%

profile of v2, /device:TPU:4, one launch (start us, length us, event | category | flops | bytes accessed | tf_op | source)
XLA Modules:
  0.0 429.0 jit_solution(14367880173726073718)
XLA Ops:
  7.2 0.0 copy-start
  7.2 0.0 all-gather.3.cloned.1.call-start
  7.2 0.8 copy-done
  8.1 1.7 convolution_convert_fusion.1
  9.8 0.0 all-gather.3.cloned.1.call-update
  9.8 0.0 all-gather.5.cloned.1.call-start
  10.5 65.4 %all-gather.3.cloned.1.call-done.src_ref = bf16[2048,256]{1,0:T(8,128)(2,1)} async-done(((bf16[256,256]{1,0:T(8,128)(2,1)}), bf16[2048,256]{1,0:T(8,128)(2,1)}) %all-gather.3.cloned.1.call-update) | async-done | bytes 1048592 | tf_op jit(solution)/shard_map/all_gather | solution.py:115
  75.9 0.0 copy-start.2
  75.9 1.2 copy-done.2
  77.1 0.0 copy-start.3
  77.1 0.7 copy-done.3
  77.8 0.0 copy-start.5
  77.8 0.7 copy-done.5
  78.5 29.9 %shard_map.94 = bf16[8192,256]{1,0:T(8,128)(2,1)S(1)} custom-call(s32[256]{0:T(256)S(1)} %bitcast.18, s32[256]{0:T(256)S(1)} %bitcast.20, s32[1]{0:T(128)} %bitcast.14.cnt_ref, bf16[256,128,128]{2,1,0:T(8,128)(2,1)} %bitcast.22, bf16[2048,256]{1,0:T(8,128)(2,1)S(1)} %copy-done.2), custom_call_target="tpu_custom_call" | custom-call | tf_op jit(solution)/shard_map/pallas_call | solution.py:72
  108.4 100.3 %all_to_all.10 = bf16[32,256,256]{2,1,0:T(8,128)(2,1)S(1)} all-to-all(bf16[32,256,256]{2,1,0:T(8,128)(2,1)S(1)} %bitcast.16), channel_id=1, replica_groups=mesh['row'=8,'col'=32] {'col'}, dimensions={0} | all-to-all | bytes 8388608 | tf_op jit(solution)/shard_map/all_to_all | solution.py:84
  208.7 0.0 copy-start.8
  208.7 0.6 convert_reduce_fusion
  209.3 0.3 copy-done.8
  209.6 0.8 multiply_convert_fusion
  210.4 0.0 all-gather.5.cloned.1.call-update
  210.4 65.2 %all-gather.5.cloned.1.call-done.src_ref = bf16[8192,256]{1,0:T(8,128)(2,1)} async-done(((bf16[256,256]{1,0:T(8,128)(2,1)}), bf16[8192,256]{1,0:T(8,128)(2,1)}) %all-gather.5.cloned.1.call-update) | async-done | bytes 4194320 | tf_op jit(solution)/shard_map/all_gather | solution.py:122
  275.6 0.0 copy-done.4
  275.6 0.0 copy-done.6
  275.6 2.2 copy-done.1
  277.8 37.3 %shard_map.95 = bf16[2048,256]{1,0:T(8,128)(2,1)S(1)} custom-call(s32[256]{0:T(256)S(1)} %bitcast.19, s32[256]{0:T(256)S(1)} %bitcast.21, s32[1]{0:T(128)} %bitcast.15.cnt_ref, bf16[256,128,128]{2,1,0:T(8,128)(2,1)} %bitcast.23, bf16[8192,256]{1,0:T(8,128)(2,1)S(1)} %copy-done.1), custom_call_target="tpu_custom_call" | custom-call | tf_op jit(solution)/shard_map/pallas_call | solution.py:72
  315.1 0.0 copy-start.7
  315.1 22.4 %all_to_all.11 = bf16[8,256,256]{2,1,0:T(8,128)(2,1)S(1)} all-to-all(bf16[8,256,256]{2,1,0:T(8,128)(2,1)S(1)} %bitcast.17), channel_id=1, replica_groups=mesh['row'=8,'col'=32] {'row'}, dimensions={0} | all-to-all | bytes 2097152 | tf_op jit(solution)/shard_map/all_to_all | solution.py:84
  337.5 0.1 reduce_sum.22
  337.7 0.2 convolution_bitcast_fusion
  337.9 1.7 collective-permute-start
  339.6 1.2 collective-permute-done
  340.8 9.9 %collective-permute-start.1 = (f32[256,256]{0,1:T(8,128)S(1)}, f32[256,256]{0,1:T(8,128)S(1)}, u32[]{:S(2)}, u32[]{:S(2)}) collective-permute-start(f32[256,256]{0,1:T(8,128)S(1)} %add.34), channel_id=1, source_target_pairs={{0,2},{1,3},{2,0},{3,1},{4,6},{5,7},{6,4},{7,5},{8,10},{9,11},{10,... | collective-permute-start | bytes 786440 | tf_op jit(solution)/shard_map/ppermute | solution.py:94
  350.8 6.6 %collective-permute-done.1 = f32[256,256]{0,1:T(8,128)S(1)} collective-permute-done((f32[256,256]{0,1:T(8,128)S(1)}, f32[256,256]{0,1:T(8,128)S(1)}, u32[]{:S(2)}, u32[]{:S(2)}) %collective-permute-start.1) | collective-permute-done | bytes 262176 | tf_op jit(solution)/shard_map/ppermute | solution.py:94
  357.4 4.0 collective-permute-start.2
  361.4 11.6 %collective-permute-done.2 = f32[256,256]{0,1:T(8,128)S(1)} collective-permute-done((f32[256,256]{0,1:T(8,128)S(1)}, f32[256,256]{0,1:T(8,128)S(1)}, u32[]{:S(2)}, u32[]{:S(2)}) %collective-permute-start.2) | collective-permute-done | bytes 262176 | tf_op jit(solution)/shard_map/ppermute | solution.py:94
  373.1 7.0 %collective-permute-start.3 = (f32[256,256]{0,1:T(8,128)S(1)}, f32[256,256]{0,1:T(8,128)S(1)}, u32[]{:S(2)}, u32[]{:S(2)}) collective-permute-start(f32[256,256]{0,1:T(8,128)S(1)} %add.36), channel_id=1, source_target_pairs={{0,8},{1,9},{2,10},{3,11},{4,12},{5,13},{6,14},{7,15},{8,0},{9,1},... | collective-permute-start | bytes 786440 | tf_op jit(solution)/shard_map/ppermute | solution.py:94
  380.1 5.6 %collective-permute-done.3 = f32[256,256]{0,1:T(8,128)S(1)} collective-permute-done((f32[256,256]{0,1:T(8,128)S(1)}, f32[256,256]{0,1:T(8,128)S(1)}, u32[]{:S(2)}, u32[]{:S(2)}) %collective-permute-start.3) | collective-permute-done | bytes 262176 | tf_op jit(solution)/shard_map/ppermute | solution.py:94
  385.7 0.1 collective-permute-start.4
  385.8 8.2 %collective-permute-done.4 = f32[256,256]{0,1:T(8,128)S(1)} collective-permute-done((f32[256,256]{0,1:T(8,128)S(1)}, f32[256,256]{0,1:T(8,128)S(1)}, u32[]{:S(2)}, u32[]{:S(2)}) %collective-permute-start.4) | collective-permute-done | bytes 262176 | tf_op jit(solution)/shard_map/ppermute | solution.py:94
  394.1 0.3 collective-permute-start.5
  394.4 7.3 %collective-permute-done.5 = f32[256,256]{0,1:T(8,128)S(1)} collective-permute-done((f32[256,256]{0,1:T(8,128)S(1)}, f32[256,256]{0,1:T(8,128)S(1)}, u32[]{:S(2)}, u32[]{:S(2)}) %collective-permute-start.5) | collective-permute-done | bytes 262176 | tf_op jit(solution)/shard_map/ppermute | solution.py:94
  401.7 0.1 collective-permute-start.6
  401.8 7.9 %collective-permute-done.6 = f32[256,256]{0,1:T(8,128)S(1)} collective-permute-done((f32[256,256]{0,1:T(8,128)S(1)}, f32[256,256]{0,1:T(8,128)S(1)}, u32[]{:S(2)}, u32[]{:S(2)}) %collective-permute-start.6) | collective-permute-done | bytes 262176 | tf_op jit(solution)/shard_map/ppermute | solution.py:94
  409.7 1.0 collective-permute-start.7
  410.7 0.0 copy-done.7
  410.7 0.9 convolution_convert_fusion
  411.6 9.7 %collective-permute-done.7 = f32[256,256]{0,1:T(8,128)S(1)} collective-permute-done((f32[256,256]{0,1:T(8,128)S(1)}, f32[256,256]{0,1:T(8,128)S(1)}, u32[]{:S(2)}, u32[]{:S(2)}) %collective-permute-start.7) | collective-permute-done | bytes 262176 | tf_op jit(solution)/shard_map/ppermute | solution.py:94
  421.3 0.8 copy.10
  (11 shorter events, 0.3 us)
Async XLA Ops:
  7.2 0.9 copy-start
  7.2 68.7 %all-gather.3.cloned.1.call-start = ((), (), s32[]{:S(2)}) async-start(), calls=%async_computation.2 | async-start | bytes 1179648 | tf_op jit(solution)/shard_map/all_gather | solution.py:115
  9.8 265.8 %all-gather.5.cloned.1.call-start = ((), (), s32[]{:S(2)}) async-start(), calls=%async_computation.3 | async-start | bytes 4325376 | tf_op jit(solution)/shard_map/all_gather | solution.py:122
  75.9 1.2 copy-start.2
  77.1 0.7 copy-start.3
  77.8 0.7 copy-start.5
  208.7 0.9 copy-start.8
  208.7 67.0 %copy-start.4 = (s32[1,256]{1,0:T(1,128)S(1)}, s32[1,256]{1,0:T(1,128)}, u32[]{:S(2)}) copy-start(s32[1,256]{1,0:T(1,128)} %param.11) | copy-start | bytes 3076
  208.7 67.0 %copy-start.6 = (s32[1,256]{1,0:T(1,128)S(1)}, s32[1,256]{1,0:T(1,128)}, u32[]{:S(2)}) copy-start(s32[1,256]{1,0:T(1,128)} %param.12) | copy-start | bytes 3076
  275.6 2.2 copy-start.1
  315.1 95.6 %copy-start.7 = (bf16[256,256]{1,0:T(8,128)(2,1)S(1)}, bf16[256,256]{1,0:T(8,128)(2,1)}, u32[]{:S(2)}) copy-start(bf16[256,256]{1,0:T(8,128)(2,1)} %param.8) | copy-start | bytes 393220
  337.9 2.9 collective-permute-start
  340.8 16.5 %collective-permute-start.1 = (f32[256,256]{0,1:T(8,128)S(1)}, f32[256,256]{0,1:T(8,128)S(1)}, u32[]{:S(2)}, u32[]{:S(2)}) collective-permute-start(f32[256,256]{0,1:T(8,128)S(1)} %add.34), channel_id=1, source_target_pairs={{0,2},{1,3},{2,0},{3,1},{4,6},{5,7},{6,4},{7,5},{8,10},{9,11},{10,... | collective-permute-start | bytes 786440 | tf_op jit(solution)/shard_map/ppermute | solution.py:94
  357.4 15.7 %collective-permute-start.2 = (f32[256,256]{0,1:T(8,128)S(1)}, f32[256,256]{0,1:T(8,128)S(1)}, u32[]{:S(2)}, u32[]{:S(2)}) collective-permute-start(f32[256,256]{0,1:T(8,128)S(1)} %add.35), channel_id=1, source_target_pairs={{0,4},{1,5},{2,6},{3,7},{4,0},{5,1},{6,2},{7,3},{8,12},{9,13},{10,... | collective-permute-start | bytes 786440 | tf_op jit(solution)/shard_map/ppermute | solution.py:94
  373.1 12.6 %collective-permute-start.3 = (f32[256,256]{0,1:T(8,128)S(1)}, f32[256,256]{0,1:T(8,128)S(1)}, u32[]{:S(2)}, u32[]{:S(2)}) collective-permute-start(f32[256,256]{0,1:T(8,128)S(1)} %add.36), channel_id=1, source_target_pairs={{0,8},{1,9},{2,10},{3,11},{4,12},{5,13},{6,14},{7,15},{8,0},{9,1},... | collective-permute-start | bytes 786440 | tf_op jit(solution)/shard_map/ppermute | solution.py:94
  385.7 8.3 %collective-permute-start.4 = (f32[256,256]{0,1:T(8,128)S(1)}, f32[256,256]{0,1:T(8,128)S(1)}, u32[]{:S(2)}, u32[]{:S(2)}) collective-permute-start(f32[256,256]{0,1:T(8,128)S(1)} %add.37), channel_id=1, source_target_pairs={{0,16},{1,17},{2,18},{3,19},{4,20},{5,21},{6,22},{7,23},{8,24},{9,... | collective-permute-start | bytes 786440 | tf_op jit(solution)/shard_map/ppermute | solution.py:94
  394.1 7.6 %collective-permute-start.5 = (f32[256,256]{0,1:T(8,128)S(1)}, f32[256,256]{0,1:T(8,128)S(1)}, u32[]{:S(2)}, u32[]{:S(2)}) collective-permute-start(f32[256,256]{0,1:T(8,128)S(1)} %add.38), channel_id=1, source_target_pairs={{0,32},{32,0},{64,96},{96,64},{128,160},{160,128},{192,224},{224,1... | collective-permute-start | bytes 786440 | tf_op jit(solution)/shard_map/ppermute | solution.py:94
  401.7 8.0 %collective-permute-start.6 = (f32[256,256]{0,1:T(8,128)S(1)}, f32[256,256]{0,1:T(8,128)S(1)}, u32[]{:S(2)}, u32[]{:S(2)}) collective-permute-start(f32[256,256]{0,1:T(8,128)S(1)} %add.39), channel_id=1, source_target_pairs={{0,64},{32,96},{64,0},{96,32},{128,192},{160,224},{192,128},{224,1... | collective-permute-start | bytes 786440 | tf_op jit(solution)/shard_map/ppermute | solution.py:94
  409.7 11.6 %collective-permute-start.7 = (f32[256,256]{0,1:T(8,128)S(1)}, f32[256,256]{0,1:T(8,128)S(1)}, u32[]{:S(2)}, u32[]{:S(2)}) collective-permute-start(f32[256,256]{0,1:T(8,128)S(1)} %add.40), channel_id=1, source_target_pairs={{0,128},{32,160},{64,192},{96,224},{128,0},{160,32},{192,64},{224,... | collective-permute-start | bytes 786440 | tf_op jit(solution)/shard_map/ppermute | solution.py:94
Sparse Core Ops, SparseCore 0:
  11.2 64.6 all-gather.2
  210.5 65.0 all-gather.4

commit v3 on v2

--- a/solution.py
+++ b/solution.py
@@ -5,7 +5,7 @@
 from jax.experimental.pallas import tpu as pltpu
 from jax.sharding import PartitionSpec as P
 
-GROUP = 16
+GROUP = 64
 
 
 def tile_product(tile_block, row_ids, col_ids, occupied, source, out_rows, transpose, out_dtype):
@@ -26,30 +26,24 @@
 
         @pl.when(g * GROUP < cnt)
         def _():
-            def body(t, carry):
+            for t in range(GROUP):
                 k = g * GROUP + t
-
-                @pl.when(k < cnt)
-                def _():
-                    r = jnp.clip(rows_ref[k], 0, row_limit)
-                    c = jnp.clip(cols_ref[k], 0, col_limit)
-                    a = tiles_ref[t]
-                    if transpose:
-                        s = src_ref[pl.ds(pl.multiple_of(r * tile_side, tile_side), tile_side), :]
-                        prod = lax.dot_general(
-                            a, s, (((0,), (0,)), ((), ())), preferred_element_type=jnp.float32
-                        )
-                        dst = c
-                    else:
-                        s = src_ref[pl.ds(pl.multiple_of(c * tile_side, tile_side), tile_side), :]
-                        prod = jnp.dot(a, s, preferred_element_type=jnp.float32)
-                        dst = r
-                    sl = pl.ds(pl.multiple_of(dst * tile_side, tile_side), tile_side)
-                    acc_ref[sl, :] += prod
-
-                return carry
-
-            lax.fori_loop(0, GROUP, body, 0, unroll=True)
+                r = jnp.clip(rows_ref[k], 0, row_limit)
+                c = jnp.clip(cols_ref[k], 0, col_limit)
+                a = tiles_ref[t]
+                if transpose:
+                    s = src_ref[pl.ds(pl.multiple_of(r * tile_side, tile_side), tile_side), :]
+                    prod = lax.dot_general(
+                        a, s, (((0,), (0,)), ((), ())), preferred_element_type=jnp.float32
+                    )
+                    dst = c
+                else:
+                    s = src_ref[pl.ds(pl.multiple_of(c * tile_side, tile_side), tile_side), :]
+                    prod = jnp.dot(a, s, preferred_element_type=jnp.float32)
+                    dst = r
+                prod = jnp.where(k < cnt, prod, 0.0)
+                sl = pl.ds(pl.multiple_of(dst * tile_side, tile_side), tile_side)
+                acc_ref[sl, :] += prod
 
         @pl.when(g == steps - 1)
         def _():

time: 430 us -> 369 us (0.86)
  Pallas kernels: 67.2 us -> 11.5 us
  starting transfers between devices: 24.2 us -> 9.33 us
  blocking collectives: 123 us -> 136 us
    pallas_call x2, Pallas kernels: 67.2 us -> 11.5 us  [tile_product(): pl.pallas_call(kernel, grid_spec=grid_spec, out_shape=jax.ShapeDtypeStruc...]
    ppermute x8, starting transfers between devices: 24.2 us -> 9.25 us  [butterfly_sum(): value = value + lax.ppermute(value, axis, pairs)]
    all_to_all x2, blocking collectives: 123 us -> 136 us  [reduce_blocks(): received = lax.all_to_all(pieces, axis, 0, 0, tiled=False)]
    all_gather x1, waiting for transfers between devices: 65.2 us -> 60.5 us  [per_device(): row_source = lax.all_gather(grad_pre, 'col', axis=0, tiled=True)]
where the time goes in v3:
time: 369 us
  waiting for transfers between devices  186 us (50%)
  blocking collectives  136 us (37%)
  between operations  14.8 us (4%)
  Pallas kernels  11.5 us (3%)
  starting transfers between devices  9.33 us (3%)
  local copies, waits for them, and re-layouts  6.79 us (2%)
    all_to_all x2, blocking collectives, reduce_blocks(): received = lax.all_to_all(pieces, axis, 0, 0, tiled=False)  136 us
    all_gather x1, waiting for transfers between devices, per_device(): column_source = lax.all_gather(projected, 'row', axis=0, tiled=True)  65.4 us
    all_gather x1, waiting for transfers between devices, per_device(): row_source = lax.all_gather(grad_pre, 'col', axis=0, tiled=True)  60.5 us
    ppermute x8, waiting for transfers between devices, butterfly_sum(): value = value + lax.ppermute(value, axis, pairs)  60.2 us
    pallas_call x2, Pallas kernels, tile_product(): pl.pallas_call(kernel, grid_spec=grid_spec, out_shape=jax.ShapeDtypeStruc...  11.5 us
    ppermute x8, starting transfers between devices, butterfly_sum(): value = value + lax.ppermute(value, axis, pairs)  9.25 us
  transfers between devices with their start and end apart: 10, of which 10 were waited for; matrix products, arithmetic and copies ran while one was open for 0% of the time, Pallas kernels for 0%

profile of v3, /device:TPU:4, one launch (start us, length us, event | category | flops | bytes accessed | tf_op | source)
XLA Modules:
  0.0 368.6 jit_solution(4217410311551813483)
XLA Ops:
  7.2 0.0 copy-start
  7.2 0.0 all-gather.3.cloned.1.call-start
  7.2 0.8 copy-done
  8.1 1.7 convolution_convert_fusion.1
  9.8 0.0 all-gather.3.cloned.1.call-update
  9.8 0.0 all-gather.5.cloned.1.call-start
  10.5 65.4 %all-gather.3.cloned.1.call-done.src_ref = bf16[2048,256]{1,0:T(8,128)(2,1)} async-done(((bf16[256,256]{1,0:T(8,128)(2,1)}), bf16[2048,256]{1,0:T(8,128)(2,1)}) %all-gather.3.cloned.1.call-update) | async-done | bytes 1048592 | tf_op jit(solution)/shard_map/all_gather | solution.py:109
  75.9 0.0 copy-start.2
  75.9 1.2 copy-done.2
  77.1 0.0 copy-start.3
  77.1 0.7 copy-done.3
  77.8 0.0 copy-start.5
  77.8 0.7 copy-done.5
  78.5 6.1 %shard_map.94 = bf16[8192,256]{1,0:T(8,128)(2,1)S(1)} custom-call(s32[256]{0:T(256)S(1)} %bitcast.18, s32[256]{0:T(256)S(1)} %bitcast.20, s32[1]{0:T(128)} %bitcast.14.cnt_ref, bf16[256,128,128]{2,1,0:T(8,128)(2,1)} %bitcast.22, bf16[2048,256]{1,0:T(8,128)(2,1)S(1)} %copy-done.2), custom_call_target="tpu_custom_call" | custom-call | tf_op jit(solution)/shard_map/pallas_call | solution.py:66
  84.5 99.7 %all_to_all.10 = bf16[32,256,256]{2,1,0:T(8,128)(2,1)S(1)} all-to-all(bf16[32,256,256]{2,1,0:T(8,128)(2,1)S(1)} %bitcast.16), channel_id=1, replica_groups=mesh['row'=8,'col'=32] {'col'}, dimensions={0} | all-to-all | bytes 8388608 | tf_op jit(solution)/shard_map/all_to_all | solution.py:78
  184.3 0.0 copy-start.8
  184.3 0.6 convert_reduce_fusion
  184.8 0.3 copy-done.8
  185.2 0.8 multiply_convert_fusion
  186.0 0.0 all-gather.5.cloned.1.call-update
  186.0 60.5 %all-gather.5.cloned.1.call-done.src_ref = bf16[8192,256]{1,0:T(8,128)(2,1)} async-done(((bf16[256,256]{1,0:T(8,128)(2,1)}), bf16[8192,256]{1,0:T(8,128)(2,1)}) %all-gather.5.cloned.1.call-update) | async-done | bytes 4194320 | tf_op jit(solution)/shard_map/all_gather | solution.py:116
  246.5 0.0 copy-done.4
  246.5 0.0 copy-done.6
  246.5 2.2 copy-done.1
  248.7 5.4 %shard_map.95 = bf16[2048,256]{1,0:T(8,128)(2,1)S(1)} custom-call(s32[256]{0:T(256)S(1)} %bitcast.19, s32[256]{0:T(256)S(1)} %bitcast.21, s32[1]{0:T(128)} %bitcast.15.cnt_ref, bf16[256,128,128]{2,1,0:T(8,128)(2,1)} %bitcast.23, bf16[8192,256]{1,0:T(8,128)(2,1)S(1)} %copy-done.1), custom_call_target="tpu_custom_call" | custom-call | tf_op jit(solution)/shard_map/pallas_call | solution.py:66
  254.1 0.0 copy-start.7
  254.1 35.8 %all_to_all.11 = bf16[8,256,256]{2,1,0:T(8,128)(2,1)S(1)} all-to-all(bf16[8,256,256]{2,1,0:T(8,128)(2,1)S(1)} %bitcast.17), channel_id=1, replica_groups=mesh['row'=8,'col'=32] {'row'}, dimensions={0} | all-to-all | bytes 2097152 | tf_op jit(solution)/shard_map/all_to_all | solution.py:78
  289.9 0.1 reduce_sum.22
  290.1 0.2 convolution_bitcast_fusion
  290.3 0.1 collective-permute-start
  290.4 1.5 collective-permute-done
  292.0 5.5 %collective-permute-start.1 = (f32[256,256]{0,1:T(8,128)S(1)}, f32[256,256]{0,1:T(8,128)S(1)}, u32[]{:S(2)}, u32[]{:S(2)}) collective-permute-start(f32[256,256]{0,1:T(8,128)S(1)} %add.34), channel_id=1, source_target_pairs={{0,2},{1,3},{2,0},{3,1},{4,6},{5,7},{6,4},{7,5},{8,10},{9,11},{10,... | collective-permute-start | bytes 786440 | tf_op jit(solution)/shard_map/ppermute | solution.py:88
  297.5 6.6 %collective-permute-done.1 = f32[256,256]{0,1:T(8,128)S(1)} collective-permute-done((f32[256,256]{0,1:T(8,128)S(1)}, f32[256,256]{0,1:T(8,128)S(1)}, u32[]{:S(2)}, u32[]{:S(2)}) %collective-permute-start.1) | collective-permute-done | bytes 262176 | tf_op jit(solution)/shard_map/ppermute | solution.py:88
  304.1 0.8 collective-permute-start.2
  304.9 13.6 %collective-permute-done.2 = f32[256,256]{0,1:T(8,128)S(1)} collective-permute-done((f32[256,256]{0,1:T(8,128)S(1)}, f32[256,256]{0,1:T(8,128)S(1)}, u32[]{:S(2)}, u32[]{:S(2)}) %collective-permute-start.2) | collective-permute-done | bytes 262176 | tf_op jit(solution)/shard_map/ppermute | solution.py:88
  318.5 0.1 collective-permute-start.3
  318.7 7.3 %collective-permute-done.3 = f32[256,256]{0,1:T(8,128)S(1)} collective-permute-done((f32[256,256]{0,1:T(8,128)S(1)}, f32[256,256]{0,1:T(8,128)S(1)}, u32[]{:S(2)}, u32[]{:S(2)}) %collective-permute-start.3) | collective-permute-done | bytes 262176 | tf_op jit(solution)/shard_map/ppermute | solution.py:88
  326.0 1.8 collective-permute-start.4
  327.8 6.2 %collective-permute-done.4 = f32[256,256]{0,1:T(8,128)S(1)} collective-permute-done((f32[256,256]{0,1:T(8,128)S(1)}, f32[256,256]{0,1:T(8,128)S(1)}, u32[]{:S(2)}, u32[]{:S(2)}) %collective-permute-start.4) | collective-permute-done | bytes 262176 | tf_op jit(solution)/shard_map/ppermute | solution.py:88
  334.1 0.1 collective-permute-start.5
  334.2 7.6 %collective-permute-done.5 = f32[256,256]{0,1:T(8,128)S(1)} collective-permute-done((f32[256,256]{0,1:T(8,128)S(1)}, f32[256,256]{0,1:T(8,128)S(1)}, u32[]{:S(2)}, u32[]{:S(2)}) %collective-permute-start.5) | collective-permute-done | bytes 262176 | tf_op jit(solution)/shard_map/ppermute | solution.py:88
  341.8 0.1 collective-permute-start.6
  341.9 7.8 %collective-permute-done.6 = f32[256,256]{0,1:T(8,128)S(1)} collective-permute-done((f32[256,256]{0,1:T(8,128)S(1)}, f32[256,256]{0,1:T(8,128)S(1)}, u32[]{:S(2)}, u32[]{:S(2)}) %collective-permute-start.6) | collective-permute-done | bytes 262176 | tf_op jit(solution)/shard_map/ppermute | solution.py:88
  349.8 0.7 collective-permute-start.7
  350.5 0.0 copy-done.7
  350.5 0.9 convolution_convert_fusion
  351.3 9.5 %collective-permute-done.7 = f32[256,256]{0,1:T(8,128)S(1)} collective-permute-done((f32[256,256]{0,1:T(8,128)S(1)}, f32[256,256]{0,1:T(8,128)S(1)}, u32[]{:S(2)}, u32[]{:S(2)}) %collective-permute-start.7) | collective-permute-done | bytes 262176 | tf_op jit(solution)/shard_map/ppermute | solution.py:88
  360.9 0.8 copy.10
  (11 shorter events, 0.3 us)
Async XLA Ops:
  7.2 0.9 copy-start
  7.2 68.7 %all-gather.3.cloned.1.call-start = ((), (), s32[]{:S(2)}) async-start(), calls=%async_computation.2 | async-start | bytes 1179648 | tf_op jit(solution)/shard_map/all_gather | solution.py:109
  9.8 236.7 %all-gather.5.cloned.1.call-start = ((), (), s32[]{:S(2)}) async-start(), calls=%async_computation.3 | async-start | bytes 4325376 | tf_op jit(solution)/shard_map/all_gather | solution.py:116
  75.9 1.2 copy-start.2
  77.1 0.7 copy-start.3
  77.8 0.7 copy-start.5
  184.3 0.9 copy-start.8
  184.3 62.3 %copy-start.4 = (s32[1,256]{1,0:T(1,128)S(1)}, s32[1,256]{1,0:T(1,128)}, u32[]{:S(2)}) copy-start(s32[1,256]{1,0:T(1,128)} %param.11) | copy-start | bytes 3076
  184.3 62.3 %copy-start.6 = (s32[1,256]{1,0:T(1,128)S(1)}, s32[1,256]{1,0:T(1,128)}, u32[]{:S(2)}) copy-start(s32[1,256]{1,0:T(1,128)} %param.12) | copy-start | bytes 3076
  246.5 2.2 copy-start.1
  254.1 96.3 %copy-start.7 = (bf16[256,256]{1,0:T(8,128)(2,1)S(1)}, bf16[256,256]{1,0:T(8,128)(2,1)}, u32[]{:S(2)}) copy-start(bf16[256,256]{1,0:T(8,128)(2,1)} %param.8) | copy-start | bytes 393220
  290.3 1.6 collective-permute-start
  292.0 12.1 %collective-permute-start.1 = (f32[256,256]{0,1:T(8,128)S(1)}, f32[256,256]{0,1:T(8,128)S(1)}, u32[]{:S(2)}, u32[]{:S(2)}) collective-permute-start(f32[256,256]{0,1:T(8,128)S(1)} %add.34), channel_id=1, source_target_pairs={{0,2},{1,3},{2,0},{3,1},{4,6},{5,7},{6,4},{7,5},{8,10},{9,11},{10,... | collective-permute-start | bytes 786440 | tf_op jit(solution)/shard_map/ppermute | solution.py:88
  304.1 14.4 %collective-permute-start.2 = (f32[256,256]{0,1:T(8,128)S(1)}, f32[256,256]{0,1:T(8,128)S(1)}, u32[]{:S(2)}, u32[]{:S(2)}) collective-permute-start(f32[256,256]{0,1:T(8,128)S(1)} %add.35), channel_id=1, source_target_pairs={{0,4},{1,5},{2,6},{3,7},{4,0},{5,1},{6,2},{7,3},{8,12},{9,13},{10,... | collective-permute-start | bytes 786440 | tf_op jit(solution)/shard_map/ppermute | solution.py:88
  318.5 7.4 %collective-permute-start.3 = (f32[256,256]{0,1:T(8,128)S(1)}, f32[256,256]{0,1:T(8,128)S(1)}, u32[]{:S(2)}, u32[]{:S(2)}) collective-permute-start(f32[256,256]{0,1:T(8,128)S(1)} %add.36), channel_id=1, source_target_pairs={{0,8},{1,9},{2,10},{3,11},{4,12},{5,13},{6,14},{7,15},{8,0},{9,1},... | collective-permute-start | bytes 786440 | tf_op jit(solution)/shard_map/ppermute | solution.py:88
  326.0 8.1 %collective-permute-start.4 = (f32[256,256]{0,1:T(8,128)S(1)}, f32[256,256]{0,1:T(8,128)S(1)}, u32[]{:S(2)}, u32[]{:S(2)}) collective-permute-start(f32[256,256]{0,1:T(8,128)S(1)} %add.37), channel_id=1, source_target_pairs={{0,16},{1,17},{2,18},{3,19},{4,20},{5,21},{6,22},{7,23},{8,24},{9,... | collective-permute-start | bytes 786440 | tf_op jit(solution)/shard_map/ppermute | solution.py:88
  334.1 7.7 %collective-permute-start.5 = (f32[256,256]{0,1:T(8,128)S(1)}, f32[256,256]{0,1:T(8,128)S(1)}, u32[]{:S(2)}, u32[]{:S(2)}) collective-permute-start(f32[256,256]{0,1:T(8,128)S(1)} %add.38), channel_id=1, source_target_pairs={{0,32},{32,0},{64,96},{96,64},{128,160},{160,128},{192,224},{224,1... | collective-permute-start | bytes 786440 | tf_op jit(solution)/shard_map/ppermute | solution.py:88
  341.8 8.0 %collective-permute-start.6 = (f32[256,256]{0,1:T(8,128)S(1)}, f32[256,256]{0,1:T(8,128)S(1)}, u32[]{:S(2)}, u32[]{:S(2)}) collective-permute-start(f32[256,256]{0,1:T(8,128)S(1)} %add.39), channel_id=1, source_target_pairs={{0,64},{32,96},{64,0},{96,32},{128,192},{160,224},{192,128},{224,1... | collective-permute-start | bytes 786440 | tf_op jit(solution)/shard_map/ppermute | solution.py:88
  349.8 11.1 %collective-permute-start.7 = (f32[256,256]{0,1:T(8,128)S(1)}, f32[256,256]{0,1:T(8,128)S(1)}, u32[]{:S(2)}, u32[]{:S(2)}) collective-permute-start(f32[256,256]{0,1:T(8,128)S(1)} %add.40), channel_id=1, source_target_pairs={{0,128},{32,160},{64,192},{96,224},{128,0},{160,32},{192,64},{224,... | collective-permute-start | bytes 786440 | tf_op jit(solution)/shard_map/ppermute | solution.py:88
Sparse Core Ops, SparseCore 0:
  11.2 64.6 all-gather.2
  186.1 60.3 all-gather.4

commit v4 on v3

--- a/solution.py
+++ b/solution.py
@@ -90,6 +90,20 @@
     return value
 
 
+def gather_pairs(value, axis):
+    size = lax.axis_size(axis)
+    me = lax.axis_index(axis)
+    step = 1
+    while step < size:
+        other = lax.ppermute(value, axis, [(i, i ^ step) for i in range(size)])
+        first = (me // step) % 2 == 0
+        value = jnp.concatenate(
+            [jnp.where(first, value, other), jnp.where(first, other, value)], axis=0
+        )
+        step *= 2
+    return value
+
+
 def silu_grad(cot_part, pre_part):
     sigma = jax.nn.sigmoid(pre_part)
     return (cot_part.astype(jnp.float32) * (sigma * (1.0 + pre_part * (1.0 - sigma)))).astype(
@@ -105,14 +119,23 @@
     row_ids = tile_rows[0]
     col_ids = tile_cols[0]
     occupied = tile_count[0, 0]
-    projected = jnp.dot(features, weight, preferred_element_type=jnp.float32).astype(jnp.bfloat16)
-    column_source = lax.all_gather(projected, "row", axis=0, tiled=True)
+    column_source = gather_pairs(features, "row")
     partial_value = tile_product(
         tile_block, row_ids, col_ids, occupied, column_source, col_devices * node_rows, False,
         jnp.bfloat16,
     )
-    pre = reduce_blocks(partial_value, "col", col_devices)
+    mixed = reduce_blocks(partial_value, "col", col_devices)
+    pre = jnp.dot(
+        mixed, weight.astype(jnp.float32), precision=lax.Precision.HIGHEST,
+        preferred_element_type=jnp.float32,
+    )
     grad_pre = silu_grad(cotangent, pre)
+    local_term = lax.dot_general(
+        mixed, grad_pre.astype(jnp.float32), (((0,), (0,)), ((), ())),
+        precision=lax.Precision.HIGHEST, preferred_element_type=jnp.float32,
+    )
+    grad_scale = float(node_rows * row_devices * col_devices) ** (-0.5)
+    weight_grad = butterfly_sum(local_term, ("col", "row")) * grad_scale
     row_source = lax.all_gather(grad_pre, "col", axis=0, tiled=True)
     output = jax.nn.silu(pre).astype(jnp.bfloat16)
     back_terms = tile_product(
@@ -124,9 +147,6 @@
     feature_grad = jnp.dot(node_grad, weight.T, preferred_element_type=jnp.float32).astype(
         jnp.bfloat16
     )
-    local_term = jnp.dot(features.T, node_grad, preferred_element_type=jnp.float32)
-    grad_scale = float(node_rows * row_devices * col_devices) ** (-0.5)
-    weight_grad = butterfly_sum(local_term, ("col", "row")) * grad_scale
     return (output, feature_grad, weight_grad)
 
 

time: 369 us -> 334 us (0.905)
  waiting for transfers between devices: 186 us -> 155 us
  blocking collectives: 136 us -> 109 us
  starting transfers between devices: 9.33 us -> 34.1 us
  local copies, waits for them, and re-layouts: 6.79 us -> 2.52 us
    all_gather x1 -> x0, waiting for transfers between devices: 65.4 us -> none  [per_device(): column_source = lax.all_gather(projected, 'row', axis=0, tiled=True)]
    all_to_all x2 -> x1, blocking collectives: 136 us -> 109 us  [reduce_blocks(): received = lax.all_to_all(pieces, axis, 0, 0, tiled=False)]
    ppermute x0 -> x3, waiting for transfers between devices: none -> 21.2 us  [gather_pairs(): other = lax.ppermute(value, axis, [(i, i ^ step) for i in range(size)])]
    ppermute x8, waiting for transfers between devices: 60.2 us -> 73.3 us  [butterfly_sum(): value = value + lax.ppermute(value, axis, pairs)]
    ppermute x0 -> x3, starting transfers between devices: none -> 12.2 us  [gather_pairs(): other = lax.ppermute(value, axis, [(i, i ^ step) for i in range(size)])]
    all_to_all x0 -> x1, starting transfers between devices: none -> 7.84 us  [reduce_blocks(): received = lax.all_to_all(pieces, axis, 0, 0, tiled=False)]
    ppermute x8, starting transfers between devices: 9.25 us -> 14 us  [butterfly_sum(): value = value + lax.ppermute(value, axis, pairs)]
    unnamed x19 -> x10, local copies, waits for them, and re-layouts: 6.79 us -> 2.52 us
  transfers between devices with their start and end apart: 10 -> 13, of which waited for: 10 -> 11; matrix products, arithmetic and copies ran while one was open for 0% -> 1% of each run, Pallas kernels for 0% -> 2%
where the time goes in v4:
time: 334 us; the launch traced here: 333 us
  waiting for transfers between devices  155 us (46%)
  blocking collectives  109 us (33%)
  starting transfers between devices  34.1 us (10%)
  between operations  14.8 us (4%)
  Pallas kernels  12.4 us (4%)
    all_to_all x1, blocking collectives, reduce_blocks(): received = lax.all_to_all(pieces, axis, 0, 0, tiled=False)  109 us
    ppermute x8, waiting for transfers between devices, butterfly_sum(): value = value + lax.ppermute(value, axis, pairs)  73.3 us
    all_gather x1, waiting for transfers between devices, per_device(): row_source = lax.all_gather(grad_pre, 'col', axis=0, tiled=True)  60 us
    ppermute x3, waiting for transfers between devices, gather_pairs(): other = lax.ppermute(value, axis, [(i, i ^ step) for i in range(size)])  21.2 us
    ppermute x8, starting transfers between devices, butterfly_sum(): value = value + lax.ppermute(value, axis, pairs)  14 us
    pallas_call x2, Pallas kernels, tile_product(): pl.pallas_call(kernel, grid_spec=grid_spec, out_shape=jax.ShapeDtypeStruc...  12.4 us
    ppermute x3, starting transfers between devices, gather_pairs(): other = lax.ppermute(value, axis, [(i, i ^ step) for i in range(size)])  12.2 us
    all_to_all x1, starting transfers between devices, reduce_blocks(): received = lax.all_to_all(pieces, axis, 0, 0, tiled=False)  7.84 us
  transfers between devices with their start and end apart: 13, of which 11 were waited for; matrix products, arithmetic and copies ran while one was open for 1% of the time, Pallas kernels for 2%

profile of v4, /device:TPU:4, one launch (start us, length us, event | category | flops | bytes accessed | tf_op | source)
XLA Modules:
  0.0 333.3 jit_solution(7519981493219499779)
XLA Ops:
  7.2 0.0 copy-start
  7.2 0.0 copy-start.3
  7.2 0.0 copy-start.2
  7.2 0.0 all-gather.2.cloned.1.call-start
  7.2 1.7 collective-permute-start
  8.9 3.9 %collective-permute-done = bf16[256,256]{1,0:T(8,128)(2,1)S(1)} collective-permute-done((bf16[256,256]{1,0:T(8,128)(2,1)}, bf16[256,256]{1,0:T(8,128)(2,1)S(1)}, u32[]{:S(2)}, u32[]{:S(2)}) %collective-permute-start) | collective-permute-done | bytes 131104 | tf_op jit(solution)/shard_map/ppermute | solution.py:98
  12.8 0.9 broadcast_select_fusion.5
  13.7 3.3 collective-permute-start.1
  17.0 5.5 %collective-permute-done.1 = bf16[512,256]{1,0:T(8,128)(2,1)S(1)} collective-permute-done((bf16[512,256]{1,0:T(8,128)(2,1)S(1)}, bf16[512,256]{1,0:T(8,128)(2,1)S(1)}, u32[]{:S(2)}, u32[]{:S(2)}) %collective-permute-start.1) | collective-permute-done | bytes 262176 | tf_op jit(solution)/shard_map/ppermute | solution.py:98
  22.5 0.1 broadcast_select_fusion.3
  22.7 7.3 %collective-permute-start.2 = (bf16[1024,256]{1,0:T(8,128)(2,1)S(1)}, bf16[1024,256]{1,0:T(8,128)(2,1)S(1)}, u32[]{:S(2)}, u32[]{:S(2)}) collective-permute-start(bf16[1024,256]{1,0:T(8,128)(2,1)S(1)} %pad_maximum_fusion.1), channel_id=1, source_target_pairs={{0,128},{32,160},{64,192},{96,224},{128,0},{160,32},{192,64},{224,... | collective-permute-start | bytes 1572872 | tf_op jit(solution)/shard_map/ppermute | solution.py:98
  30.6 11.8 %collective-permute-done.2 = bf16[1024,256]{1,0:T(8,128)(2,1)S(1)} collective-permute-done((bf16[1024,256]{1,0:T(8,128)(2,1)S(1)}, bf16[1024,256]{1,0:T(8,128)(2,1)S(1)}, u32[]{:S(2)}, u32[]{:S(2)}) %collective-permute-start.2) | collective-permute-done | bytes 524320 | tf_op jit(solution)/shard_map/ppermute | solution.py:98
  42.4 0.2 broadcast_select_fusion.1
  42.7 0.1 pad_maximum_fusion.src_ref
  42.7 0.0 copy-done.3
  42.8 0.0 copy-done.2
  42.8 6.1 %shard_map.94 = bf16[8192,256]{1,0:T(8,128)(2,1)S(1)} custom-call(s32[256]{0:T(256)S(1)} %bitcast.15, s32[256]{0:T(256)S(1)} %bitcast.17, s32[1]{0:T(128)} %bitcast.12.cnt_ref, bf16[256,128,128]{2,1,0:T(8,128)(2,1)} %bitcast.19, bf16[2048,256]{1,0:T(8,128)(2,1)S(1)} %pad_maximum_fusion.src_ref), custom_call_target="tpu_custom_call" | custom-call | tf_op jit(solution)/shard_map/pallas_call | solution.py:66
  48.8 108.6 %all_to_all.10 = bf16[32,256,256]{2,1,0:T(8,128)(2,1)S(1)} all-to-all(bf16[32,256,256]{2,1,0:T(8,128)(2,1)S(1)} %bitcast.14), channel_id=1, replica_groups=mesh['row'=8,'col'=32] {'col'}, dimensions={0} | all-to-all | bytes 8388608 | tf_op jit(solution)/shard_map/all_to_all | solution.py:78
  157.4 0.6 convert_reduce_fusion
  158.0 0.0 copy-done
  158.0 0.3 copy-done.4
  158.3 1.0 multiply_convert_fusion
  159.4 0.0 all-gather.2.cloned.1.call-update
  159.4 1.3 fusion
  160.7 1.2 collective-permute-start.3
  161.9 1.2 collective-permute-done.3
  163.1 0.1 collective-permute-start.4
  163.2 60.0 %all-gather.2.cloned.1.call-done.src_ref = bf16[8192,256]{1,0:T(8,128)(2,1)} async-done(((bf16[256,256]{1,0:T(8,128)(2,1)}), bf16[8192,256]{1,0:T(8,128)(2,1)}) %all-gather.2.cloned.1.call-update) | async-done | bytes 4194320 | tf_op jit(solution)/shard_map/all_gather | solution.py:139
  223.2 2.2 copy-done.1
  225.4 6.4 %shard_map.95 = bf16[2048,256]{1,0:T(8,128)(2,1)} custom-call(s32[256]{0:T(256)S(1)} %bitcast.16, s32[256]{0:T(256)S(1)} %bitcast.18, s32[1]{0:T(128)} %bitcast.13.cnt_ref, bf16[256,128,128]{2,1,0:T(8,128)(2,1)} %bitcast.20, bf16[8192,256]{1,0:T(8,128)(2,1)S(1)} %copy-done.1), custom_call_target="tpu_custom_call" | custom-call | tf_op jit(solution)/shard_map/pallas_call | solution.py:66
  231.7 7.8 %all-to-all-start.1 = ((bf16[8,256,256]{2,1,0:T(8,128)(2,1)}), bf16[8,256,256]{2,1,0:T(8,128)(2,1)S(1)}, u32[]{:S(2)}, u32[]{:S(2)}) async-start(bf16[8,256,256]{2,1,0:T(8,128)(2,1)} %bitcast.5), calls=%async_computation.1 | async-start | bytes 2097152 | tf_op jit(solution)/shard_map/all_to_all | solution.py:78
  239.6 0.0 collective-permute-done.4
  239.6 1.6 collective-permute-start.5
  241.2 35.8 %collective-permute-done.5 = f32[256,256]{1,0:T(8,128)S(1)} collective-permute-done((f32[256,256]{1,0:T(8,128)S(1)}, f32[256,256]{1,0:T(8,128)S(1)}, u32[]{:S(2)}, u32[]{:S(2)}) %collective-permute-start.5) | collective-permute-done | bytes 262176 | tf_op jit(solution)/shard_map/ppermute | solution.py:88
  277.1 0.1 collective-permute-start.6
  277.2 8.3 %collective-permute-done.6 = f32[256,256]{1,0:T(8,128)S(1)} collective-permute-done((f32[256,256]{1,0:T(8,128)S(1)}, f32[256,256]{1,0:T(8,128)S(1)}, u32[]{:S(2)}, u32[]{:S(2)}) %collective-permute-start.6) | collective-permute-done | bytes 262176 | tf_op jit(solution)/shard_map/ppermute | solution.py:88
  285.5 1.6 collective-permute-start.7
  287.1 7.5 %collective-permute-done.7 = f32[256,256]{1,0:T(8,128)S(1)} collective-permute-done((f32[256,256]{1,0:T(8,128)S(1)}, f32[256,256]{1,0:T(8,128)S(1)}, u32[]{:S(2)}, u32[]{:S(2)}) %collective-permute-start.7) | collective-permute-done | bytes 262176 | tf_op jit(solution)/shard_map/ppermute | solution.py:88
  294.6 2.1 collective-permute-start.8
  296.7 4.9 %collective-permute-done.8 = f32[256,256]{1,0:T(8,128)S(1)} collective-permute-done((f32[256,256]{1,0:T(8,128)S(1)}, f32[256,256]{1,0:T(8,128)S(1)}, u32[]{:S(2)}, u32[]{:S(2)}) %collective-permute-start.8) | collective-permute-done | bytes 262176 | tf_op jit(solution)/shard_map/ppermute | solution.py:88
  301.6 3.3 collective-permute-start.9
  305.0 4.6 %collective-permute-done.9 = f32[256,256]{1,0:T(8,128)S(1)} collective-permute-done((f32[256,256]{1,0:T(8,128)S(1)}, f32[256,256]{1,0:T(8,128)S(1)}, u32[]{:S(2)}, u32[]{:S(2)}) %collective-permute-start.9) | collective-permute-done | bytes 262176 | tf_op jit(solution)/shard_map/ppermute | solution.py:88
  309.6 4.0 %collective-permute-start.10 = (f32[256,256]{1,0:T(8,128)S(1)}, f32[256,256]{1,0:T(8,128)S(1)}, u32[]{:S(2)}, u32[]{:S(2)}) collective-permute-start(f32[256,256]{1,0:T(8,128)S(1)} %add.56), channel_id=1, source_target_pairs={{0,128},{32,160},{64,192},{96,224},{128,0},{160,32},{192,64},{224,... | collective-permute-start | bytes 786440 | tf_op jit(solution)/shard_map/ppermute | solution.py:88
  313.7 11.1 %collective-permute-done.10 = f32[256,256]{1,0:T(8,128)S(1)} collective-permute-done((f32[256,256]{1,0:T(8,128)S(1)}, f32[256,256]{1,0:T(8,128)S(1)}, u32[]{:S(2)}, u32[]{:S(2)}) %collective-permute-start.10) | collective-permute-done | bytes 262176 | tf_op jit(solution)/shard_map/ppermute | solution.py:88
  324.7 0.7 add_multiply_fusion
  325.4 0.0 all-to-all-done.1
  325.4 0.1 reduce_sum.22
  325.6 0.9 convolution_convert_fusion
  (11 shorter events, 0.3 us)
Async XLA Ops:
  7.2 150.8 %copy-start = (bf16[256,256]{1,0:T(8,128)(2,1)S(1)}, bf16[256,256]{1,0:T(8,128)(2,1)}, u32[]{:S(2)}) copy-start(bf16[256,256]{1,0:T(8,128)(2,1)} %param.8) | copy-start | bytes 393220
  7.2 35.6 %copy-start.3 = (s32[1,256]{1,0:T(1,128)S(1)}, s32[1,256]{1,0:T(1,128)}, u32[]{:S(2)}) copy-start(s32[1,256]{1,0:T(1,128)} %param.12) | copy-start | bytes 3076
  7.2 35.6 %copy-start.2 = (s32[1,256]{1,0:T(1,128)S(1)}, s32[1,256]{1,0:T(1,128)}, u32[]{:S(2)}) copy-start(s32[1,256]{1,0:T(1,128)} %param.11) | copy-start | bytes 3076
  7.2 216.0 %all-gather.2.cloned.1.call-start = ((), (), s32[]{:S(2)}) async-start(), calls=%async_computation.2 | async-start | bytes 4325376 | tf_op jit(solution)/shard_map/all_gather | solution.py:139
  7.2 5.5 %collective-permute-start = (bf16[256,256]{1,0:T(8,128)(2,1)}, bf16[256,256]{1,0:T(8,128)(2,1)S(1)}, u32[]{:S(2)}, u32[]{:S(2)}) collective-permute-start(bf16[256,256]{1,0:T(8,128)(2,1)} %param.7), channel_id=1, source_target_pairs={{0,32},{32,0},{64,96},{96,64},{128,160},{160,128},{192,224},{224,1... | collective-permute-start | bytes 393224 | tf_op jit(solution)/shard_map/ppermute | solution.py:98
  13.7 8.8 %collective-permute-start.1 = (bf16[512,256]{1,0:T(8,128)(2,1)S(1)}, bf16[512,256]{1,0:T(8,128)(2,1)S(1)}, u32[]{:S(2)}, u32[]{:S(2)}) collective-permute-start(bf16[512,256]{1,0:T(8,128)(2,1)S(1)} %pad_maximum_fusion.2), channel_id=1, source_target_pairs={{0,64},{32,96},{64,0},{96,32},{128,192},{160,224},{192,128},{224,1... | collective-permute-start | bytes 786440 | tf_op jit(solution)/shard_map/ppermute | solution.py:98
  22.7 19.8 %collective-permute-start.2 = (bf16[1024,256]{1,0:T(8,128)(2,1)S(1)}, bf16[1024,256]{1,0:T(8,128)(2,1)S(1)}, u32[]{:S(2)}, u32[]{:S(2)}) collective-permute-start(bf16[1024,256]{1,0:T(8,128)(2,1)S(1)} %pad_maximum_fusion.1), channel_id=1, source_target_pairs={{0,128},{32,160},{64,192},{96,224},{128,0},{160,32},{192,64},{224,... | collective-permute-start | bytes 1572872 | tf_op jit(solution)/shard_map/ppermute | solution.py:98
  157.4 0.9 copy-start.4
  160.7 2.3 collective-permute-start.3
  163.1 76.5 %collective-permute-start.4 = (f32[256,256]{1,0:T(8,128)S(1)}, f32[256,256]{1,0:T(8,128)S(1)}, u32[]{:S(2)}, u32[]{:S(2)}) collective-permute-start(f32[256,256]{1,0:T(8,128)S(1)} %add.50), channel_id=1, source_target_pairs={{0,2},{1,3},{2,0},{3,1},{4,6},{5,7},{6,4},{7,5},{8,10},{9,11},{10,... | collective-permute-start | bytes 786440 | tf_op jit(solution)/shard_map/ppermute | solution.py:88
  223.2 2.2 copy-start.1
  231.7 93.7 %all-to-all-start.1 = ((bf16[8,256,256]{2,1,0:T(8,128)(2,1)}), bf16[8,256,256]{2,1,0:T(8,128)(2,1)S(1)}, u32[]{:S(2)}, u32[]{:S(2)}) async-start(bf16[8,256,256]{2,1,0:T(8,128)(2,1)} %bitcast.5), calls=%async_computation.1 | async-start | bytes 2097152 | tf_op jit(solution)/shard_map/all_to_all | solution.py:78
  239.6 37.4 %collective-permute-start.5 = (f32[256,256]{1,0:T(8,128)S(1)}, f32[256,256]{1,0:T(8,128)S(1)}, u32[]{:S(2)}, u32[]{:S(2)}) collective-permute-start(f32[256,256]{1,0:T(8,128)S(1)} %add.51), channel_id=1, source_target_pairs={{0,4},{1,5},{2,6},{3,7},{4,0},{5,1},{6,2},{7,3},{8,12},{9,13},{10,... | collective-permute-start | bytes 786440 | tf_op jit(solution)/shard_map/ppermute | solution.py:88
  277.1 8.4 %collective-permute-start.6 = (f32[256,256]{1,0:T(8,128)S(1)}, f32[256,256]{1,0:T(8,128)S(1)}, u32[]{:S(2)}, u32[]{:S(2)}) collective-permute-start(f32[256,256]{1,0:T(8,128)S(1)} %add.52), channel_id=1, source_target_pairs={{0,8},{1,9},{2,10},{3,11},{4,12},{5,13},{6,14},{7,15},{8,0},{9,1},... | collective-permute-start | bytes 786440 | tf_op jit(solution)/shard_map/ppermute | solution.py:88
  285.5 9.1 %collective-permute-start.7 = (f32[256,256]{1,0:T(8,128)S(1)}, f32[256,256]{1,0:T(8,128)S(1)}, u32[]{:S(2)}, u32[]{:S(2)}) collective-permute-start(f32[256,256]{1,0:T(8,128)S(1)} %add.53), channel_id=1, source_target_pairs={{0,16},{1,17},{2,18},{3,19},{4,20},{5,21},{6,22},{7,23},{8,24},{9,... | collective-permute-start | bytes 786440 | tf_op jit(solution)/shard_map/ppermute | solution.py:88
  294.6 7.0 %collective-permute-start.8 = (f32[256,256]{1,0:T(8,128)S(1)}, f32[256,256]{1,0:T(8,128)S(1)}, u32[]{:S(2)}, u32[]{:S(2)}) collective-permute-start(f32[256,256]{1,0:T(8,128)S(1)} %add.54), channel_id=1, source_target_pairs={{0,32},{32,0},{64,96},{96,64},{128,160},{160,128},{192,224},{224,1... | collective-permute-start | bytes 786440 | tf_op jit(solution)/shard_map/ppermute | solution.py:88
  301.6 8.0 %collective-permute-start.9 = (f32[256,256]{1,0:T(8,128)S(1)}, f32[256,256]{1,0:T(8,128)S(1)}, u32[]{:S(2)}, u32[]{:S(2)}) collective-permute-start(f32[256,256]{1,0:T(8,128)S(1)} %add.55), channel_id=1, source_target_pairs={{0,64},{32,96},{64,0},{96,32},{128,192},{160,224},{192,128},{224,1... | collective-permute-start | bytes 786440 | tf_op jit(solution)/shard_map/ppermute | solution.py:88
  309.6 15.1 %collective-permute-start.10 = (f32[256,256]{1,0:T(8,128)S(1)}, f32[256,256]{1,0:T(8,128)S(1)}, u32[]{:S(2)}, u32[]{:S(2)}) collective-permute-start(f32[256,256]{1,0:T(8,128)S(1)} %add.56), channel_id=1, source_target_pairs={{0,128},{32,160},{64,192},{96,224},{128,0},{160,32},{192,64},{224,... | collective-permute-start | bytes 786440 | tf_op jit(solution)/shard_map/ppermute | solution.py:88
Sparse Core Ops, SparseCore 0:
  159.5 63.6 all-gather.1

commit v5 on v4

--- a/solution.py
+++ b/solution.py
@@ -135,13 +135,15 @@
         precision=lax.Precision.HIGHEST, preferred_element_type=jnp.float32,
     )
     grad_scale = float(node_rows * row_devices * col_devices) ** (-0.5)
-    weight_grad = butterfly_sum(local_term, ("col", "row")) * grad_scale
+    row_summed = butterfly_sum(local_term, ("row",))
     row_source = lax.all_gather(grad_pre, "col", axis=0, tiled=True)
+    row_source, row_summed = lax.optimization_barrier((row_source, row_summed))
     output = jax.nn.silu(pre).astype(jnp.bfloat16)
     back_terms = tile_product(
         tile_block, row_ids, col_ids, occupied, row_source, row_devices * node_rows, True,
         jnp.bfloat16,
     )
+    weight_grad = butterfly_sum(row_summed, ("col",)) * grad_scale
     aggregated = reduce_blocks(back_terms, "row", row_devices)
     node_grad = aggregated.astype(jnp.bfloat16)
     feature_grad = jnp.dot(node_grad, weight.T, preferred_element_type=jnp.float32).astype(

time: 334 us -> 324 us (0.970); the launches traced: 333 us -> 320 us
  waiting for transfers between devices: 155 us -> 133 us
  starting transfers between devices: 34.1 us -> 43.7 us
    all_gather x1, waiting for transfers between devices: 60 us -> 34 us  [per_device(): row_source = lax.all_gather(grad_pre, 'col', axis=0, tiled=True)]
    all_to_all x1, starting transfers between devices: 7.84 us -> 12.9 us  [reduce_blocks(): received = lax.all_to_all(pieces, axis, 0, 0, tiled=False)]
    ppermute x8, starting transfers between devices: 14 us -> 18.5 us  [butterfly_sum(): value = value + lax.ppermute(value, axis, pairs)]
    ppermute x8, waiting for transfers between devices: 73.3 us -> 77.5 us  [butterfly_sum(): value = value + lax.ppermute(value, axis, pairs)]
  transfers between devices with their start and end apart: 13 -> 13, of which waited for: 11 -> 12; matrix products, arithmetic and copies ran while one was open for 1% -> 1% of each run, Pallas kernels for 2% -> 0%
where the time goes in v5:
time: 324 us; the launch traced here: 320 us
  waiting for transfers between devices  133 us (41%)
  blocking collectives  110 us (34%)
  starting transfers between devices  43.7 us (13%)
  between operations  14.8 us (5%)
  Pallas kernels  9.63 us (3%)
    all_to_all x1, blocking collectives, reduce_blocks(): received = lax.all_to_all(pieces, axis, 0, 0, tiled=False)  110 us
    ppermute x8, waiting for transfers between devices, butterfly_sum(): value = value + lax.ppermute(value, axis, pairs)  77.5 us
    all_gather x1, waiting for transfers between devices, per_device(): row_source = lax.all_gather(grad_pre, 'col', axis=0, tiled=True)  34 us
    ppermute x3, waiting for transfers between devices, gather_pairs(): other = lax.ppermute(value, axis, [(i, i ^ step) for i in range(size)])  21.2 us
    ppermute x8, starting transfers between devices, butterfly_sum(): value = value + lax.ppermute(value, axis, pairs)  18.5 us
    all_to_all x1, starting transfers between devices, reduce_blocks(): received = lax.all_to_all(pieces, axis, 0, 0, tiled=False)  12.9 us
    ppermute x3, starting transfers between devices, gather_pairs(): other = lax.ppermute(value, axis, [(i, i ^ step) for i in range(size)])  12.2 us
    pallas_call x2, Pallas kernels, tile_product(): pl.pallas_call(kernel, grid_spec=grid_spec, out_shape=jax.ShapeDtypeStruc...  9.63 us
  transfers between devices with their start and end apart: 13, of which 12 were waited for; matrix products, arithmetic and copies ran while one was open for 1% of the time, Pallas kernels for 0%

profile of v5, /device:TPU:4, one launch (start us, length us, event | category | flops | bytes accessed | tf_op | source)
XLA Modules:
  0.0 319.7 jit_solution(5421990959217725962)
XLA Ops:
  7.2 0.0 copy-start
  7.2 0.0 copy-start.3
  7.2 0.0 copy-start.2
  7.2 0.0 all-gather.2.cloned.1.call-start
  7.2 1.7 collective-permute-start
  8.9 3.9 %collective-permute-done = bf16[256,256]{1,0:T(8,128)(2,1)S(1)} collective-permute-done((bf16[256,256]{1,0:T(8,128)(2,1)}, bf16[256,256]{1,0:T(8,128)(2,1)S(1)}, u32[]{:S(2)}, u32[]{:S(2)}) %collective-permute-start) | collective-permute-done | bytes 131104 | tf_op jit(solution)/shard_map/ppermute | solution.py:98
  12.8 0.9 broadcast_select_fusion.5
  13.7 3.3 %collective-permute-start.1 = (bf16[512,256]{1,0:T(8,128)(2,1)S(1)}, bf16[512,256]{1,0:T(8,128)(2,1)S(1)}, u32[]{:S(2)}, u32[]{:S(2)}) collective-permute-start(bf16[512,256]{1,0:T(8,128)(2,1)S(1)} %pad_maximum_fusion.2), channel_id=1, source_target_pairs={{0,64},{32,96},{64,0},{96,32},{128,192},{160,224},{192,128},{224,1... | collective-permute-start | bytes 786440 | tf_op jit(solution)/shard_map/ppermute | solution.py:98
  17.0 5.5 %collective-permute-done.1 = bf16[512,256]{1,0:T(8,128)(2,1)S(1)} collective-permute-done((bf16[512,256]{1,0:T(8,128)(2,1)S(1)}, bf16[512,256]{1,0:T(8,128)(2,1)S(1)}, u32[]{:S(2)}, u32[]{:S(2)}) %collective-permute-start.1) | collective-permute-done | bytes 262176 | tf_op jit(solution)/shard_map/ppermute | solution.py:98
  22.5 0.1 broadcast_select_fusion.3
  22.7 7.3 %collective-permute-start.2 = (bf16[1024,256]{1,0:T(8,128)(2,1)S(1)}, bf16[1024,256]{1,0:T(8,128)(2,1)S(1)}, u32[]{:S(2)}, u32[]{:S(2)}) collective-permute-start(bf16[1024,256]{1,0:T(8,128)(2,1)S(1)} %pad_maximum_fusion.1), channel_id=1, source_target_pairs={{0,128},{32,160},{64,192},{96,224},{128,0},{160,32},{192,64},{224,... | collective-permute-start | bytes 1572872 | tf_op jit(solution)/shard_map/ppermute | solution.py:98
  30.6 11.8 %collective-permute-done.2 = bf16[1024,256]{1,0:T(8,128)(2,1)S(1)} collective-permute-done((bf16[1024,256]{1,0:T(8,128)(2,1)S(1)}, bf16[1024,256]{1,0:T(8,128)(2,1)S(1)}, u32[]{:S(2)}, u32[]{:S(2)}) %collective-permute-start.2) | collective-permute-done | bytes 524320 | tf_op jit(solution)/shard_map/ppermute | solution.py:98
  42.4 0.2 broadcast_select_fusion.1
  42.7 0.1 pad_maximum_fusion.src_ref
  42.7 0.0 copy-done.3
  42.8 0.0 copy-done.2
  42.8 4.7 %shard_map.94 = bf16[8192,256]{1,0:T(8,128)(2,1)S(1)} custom-call(s32[256]{0:T(256)S(1)} %bitcast.15, s32[256]{0:T(256)S(1)} %bitcast.17, s32[1]{0:T(128)} %bitcast.12.cnt_ref, bf16[256,128,128]{2,1,0:T(8,128)(2,1)} %bitcast.19, bf16[2048,256]{1,0:T(8,128)(2,1)S(1)} %pad_maximum_fusion.src_ref), custom_call_target="tpu_custom_call" | custom-call | tf_op jit(solution)/shard_map/pallas_call | solution.py:66
  47.4 110.0 %all_to_all.10 = bf16[32,256,256]{2,1,0:T(8,128)(2,1)S(1)} all-to-all(bf16[32,256,256]{2,1,0:T(8,128)(2,1)S(1)} %bitcast.14), channel_id=1, replica_groups=mesh['row'=8,'col'=32] {'col'}, dimensions={0} | all-to-all | bytes 8388608 | tf_op jit(solution)/shard_map/all_to_all | solution.py:78
  157.4 0.6 convert_reduce_fusion
  158.0 0.0 copy-done
  158.0 0.3 copy-done.4
  158.3 1.0 multiply_convert_fusion
  159.4 0.0 all-gather.2.cloned.1.call-update
  159.4 1.3 fusion
  160.7 3.6 %collective-permute-start.3 = (f32[256,256]{1,0:T(8,128)S(1)}, f32[256,256]{1,0:T(8,128)S(1)}, u32[]{:S(2)}, u32[]{:S(2)}) collective-permute-start(f32[256,256]{1,0:T(8,128)S(1)} %fusion), channel_id=1, source_target_pairs={{0,32},{32,0},{64,96},{96,64},{128,160},{160,128},{192,224},{224,1... | collective-permute-start | bytes 786440 | tf_op jit(solution)/shard_map/ppermute | solution.py:88
  164.3 6.8 %collective-permute-done.3 = f32[256,256]{1,0:T(8,128)S(1)} collective-permute-done((f32[256,256]{1,0:T(8,128)S(1)}, f32[256,256]{1,0:T(8,128)S(1)}, u32[]{:S(2)}, u32[]{:S(2)}) %collective-permute-start.3) | collective-permute-done | bytes 262176 | tf_op jit(solution)/shard_map/ppermute | solution.py:88
  171.1 4.0 %collective-permute-start.4 = (f32[256,256]{1,0:T(8,128)S(1)}, f32[256,256]{1,0:T(8,128)S(1)}, u32[]{:S(2)}, u32[]{:S(2)}) collective-permute-start(f32[256,256]{1,0:T(8,128)S(1)} %add.50), channel_id=1, source_target_pairs={{0,64},{32,96},{64,0},{96,32},{128,192},{160,224},{192,128},{224,1... | collective-permute-start | bytes 786440 | tf_op jit(solution)/shard_map/ppermute | solution.py:88
  175.1 6.6 %collective-permute-done.4 = f32[256,256]{1,0:T(8,128)S(1)} collective-permute-done((f32[256,256]{1,0:T(8,128)S(1)}, f32[256,256]{1,0:T(8,128)S(1)}, u32[]{:S(2)}, u32[]{:S(2)}) %collective-permute-start.4) | collective-permute-done | bytes 262176 | tf_op jit(solution)/shard_map/ppermute | solution.py:88
  181.7 4.0 %collective-permute-start.5 = (f32[256,256]{1,0:T(8,128)S(1)}, f32[256,256]{1,0:T(8,128)S(1)}, u32[]{:S(2)}, u32[]{:S(2)}) collective-permute-start(f32[256,256]{1,0:T(8,128)S(1)} %add.51), channel_id=1, source_target_pairs={{0,128},{32,160},{64,192},{96,224},{128,0},{160,32},{192,64},{224,... | collective-permute-start | bytes 786440 | tf_op jit(solution)/shard_map/ppermute | solution.py:88
  185.8 13.3 %collective-permute-done.5 = f32[256,256]{1,0:T(8,128)S(1)} collective-permute-done((f32[256,256]{1,0:T(8,128)S(1)}, f32[256,256]{1,0:T(8,128)S(1)}, u32[]{:S(2)}, u32[]{:S(2)}) %collective-permute-start.5) | collective-permute-done | bytes 262176 | tf_op jit(solution)/shard_map/ppermute | solution.py:88
  199.1 34.0 %all-gather.2.cloned.1.call-done.src_ref = bf16[8192,256]{1,0:T(8,128)(2,1)} async-done(((bf16[256,256]{1,0:T(8,128)(2,1)}), bf16[8192,256]{1,0:T(8,128)(2,1)}) %all-gather.2.cloned.1.call-update) | async-done | bytes 4194320 | tf_op jit(solution)/shard_map/all_gather | solution.py:139
  233.1 2.2 copy-done.1
  235.3 5.0 %shard_map.95 = bf16[2048,256]{1,0:T(8,128)(2,1)} custom-call(s32[256]{0:T(256)S(1)} %bitcast.16, s32[256]{0:T(256)S(1)} %bitcast.18, s32[1]{0:T(128)} %bitcast.13.cnt_ref, bf16[256,128,128]{2,1,0:T(8,128)(2,1)} %bitcast.20, bf16[8192,256]{1,0:T(8,128)(2,1)S(1)} %copy-done.1), custom_call_target="tpu_custom_call" | custom-call | tf_op jit(solution)/shard_map/pallas_call | solution.py:66
  240.3 12.9 %all-to-all-start.1 = ((bf16[8,256,256]{2,1,0:T(8,128)(2,1)}), bf16[8,256,256]{2,1,0:T(8,128)(2,1)S(1)}, u32[]{:S(2)}, u32[]{:S(2)}) async-start(bf16[8,256,256]{2,1,0:T(8,128)(2,1)} %bitcast.5), calls=%async_computation.1 | async-start | bytes 2097152 | tf_op jit(solution)/shard_map/all_to_all | solution.py:78
  253.2 0.0 collective-permute-start.6
  253.2 1.5 collective-permute-done.6
  254.8 0.1 collective-permute-start.7
  254.9 24.3 %collective-permute-done.7 = f32[256,256]{1,0:T(8,128)S(1)} collective-permute-done((f32[256,256]{1,0:T(8,128)S(1)}, f32[256,256]{1,0:T(8,128)S(1)}, u32[]{:S(2)}, u32[]{:S(2)}) %collective-permute-start.7) | collective-permute-done | bytes 262176 | tf_op jit(solution)/shard_map/ppermute | solution.py:88
  279.2 2.0 collective-permute-start.8
  281.2 12.5 %collective-permute-done.8 = f32[256,256]{1,0:T(8,128)S(1)} collective-permute-done((f32[256,256]{1,0:T(8,128)S(1)}, f32[256,256]{1,0:T(8,128)S(1)}, u32[]{:S(2)}, u32[]{:S(2)}) %collective-permute-start.8) | collective-permute-done | bytes 262176 | tf_op jit(solution)/shard_map/ppermute | solution.py:88
  293.7 1.5 collective-permute-start.9
  295.2 6.5 %collective-permute-done.9 = f32[256,256]{1,0:T(8,128)S(1)} collective-permute-done((f32[256,256]{1,0:T(8,128)S(1)}, f32[256,256]{1,0:T(8,128)S(1)}, u32[]{:S(2)}, u32[]{:S(2)}) %collective-permute-start.9) | collective-permute-done | bytes 262176 | tf_op jit(solution)/shard_map/ppermute | solution.py:88
  301.7 3.4 %collective-permute-start.10 = (f32[256,256]{1,0:T(8,128)S(1)}, f32[256,256]{1,0:T(8,128)S(1)}, u32[]{:S(2)}, u32[]{:S(2)}) collective-permute-start(f32[256,256]{1,0:T(8,128)S(1)} %add.56), channel_id=1, source_target_pairs={{0,16},{1,17},{2,18},{3,19},{4,20},{5,21},{6,22},{7,23},{8,24},{9,... | collective-permute-start | bytes 786440 | tf_op jit(solution)/shard_map/ppermute | solution.py:88
  305.1 6.0 %collective-permute-done.10 = f32[256,256]{1,0:T(8,128)S(1)} collective-permute-done((f32[256,256]{1,0:T(8,128)S(1)}, f32[256,256]{1,0:T(8,128)S(1)}, u32[]{:S(2)}, u32[]{:S(2)}) %collective-permute-start.10) | collective-permute-done | bytes 262176 | tf_op jit(solution)/shard_map/ppermute | solution.py:88
  311.1 0.7 add_multiply_fusion
  311.8 0.0 all-to-all-done.1
  311.8 0.1 reduce_sum.22
  311.9 0.9 convolution_convert_fusion
  (11 shorter events, 0.3 us)
Async XLA Ops:
  7.2 150.8 %copy-start = (bf16[256,256]{1,0:T(8,128)(2,1)S(1)}, bf16[256,256]{1,0:T(8,128)(2,1)}, u32[]{:S(2)}) copy-start(bf16[256,256]{1,0:T(8,128)(2,1)} %param.8) | copy-start | bytes 393220
  7.2 35.6 %copy-start.3 = (s32[1,256]{1,0:T(1,128)S(1)}, s32[1,256]{1,0:T(1,128)}, u32[]{:S(2)}) copy-start(s32[1,256]{1,0:T(1,128)} %param.12) | copy-start | bytes 3076
  7.2 35.6 %copy-start.2 = (s32[1,256]{1,0:T(1,128)S(1)}, s32[1,256]{1,0:T(1,128)}, u32[]{:S(2)}) copy-start(s32[1,256]{1,0:T(1,128)} %param.11) | copy-start | bytes 3076
  7.2 225.9 %all-gather.2.cloned.1.call-start = ((), (), s32[]{:S(2)}) async-start(), calls=%async_computation.2 | async-start | bytes 4325376 | tf_op jit(solution)/shard_map/all_gather | solution.py:139
  7.2 5.5 %collective-permute-start = (bf16[256,256]{1,0:T(8,128)(2,1)}, bf16[256,256]{1,0:T(8,128)(2,1)S(1)}, u32[]{:S(2)}, u32[]{:S(2)}) collective-permute-start(bf16[256,256]{1,0:T(8,128)(2,1)} %param.7), channel_id=1, source_target_pairs={{0,32},{32,0},{64,96},{96,64},{128,160},{160,128},{192,224},{224,1... | collective-permute-start | bytes 393224 | tf_op jit(solution)/shard_map/ppermute | solution.py:98
  13.7 8.8 %collective-permute-start.1 = (bf16[512,256]{1,0:T(8,128)(2,1)S(1)}, bf16[512,256]{1,0:T(8,128)(2,1)S(1)}, u32[]{:S(2)}, u32[]{:S(2)}) collective-permute-start(bf16[512,256]{1,0:T(8,128)(2,1)S(1)} %pad_maximum_fusion.2), channel_id=1, source_target_pairs={{0,64},{32,96},{64,0},{96,32},{128,192},{160,224},{192,128},{224,1... | collective-permute-start | bytes 786440 | tf_op jit(solution)/shard_map/ppermute | solution.py:98
  22.7 19.8 %collective-permute-start.2 = (bf16[1024,256]{1,0:T(8,128)(2,1)S(1)}, bf16[1024,256]{1,0:T(8,128)(2,1)S(1)}, u32[]{:S(2)}, u32[]{:S(2)}) collective-permute-start(bf16[1024,256]{1,0:T(8,128)(2,1)S(1)} %pad_maximum_fusion.1), channel_id=1, source_target_pairs={{0,128},{32,160},{64,192},{96,224},{128,0},{160,32},{192,64},{224,... | collective-permute-start | bytes 1572872 | tf_op jit(solution)/shard_map/ppermute | solution.py:98
  157.4 0.9 copy-start.4
  160.7 10.3 %collective-permute-start.3 = (f32[256,256]{1,0:T(8,128)S(1)}, f32[256,256]{1,0:T(8,128)S(1)}, u32[]{:S(2)}, u32[]{:S(2)}) collective-permute-start(f32[256,256]{1,0:T(8,128)S(1)} %fusion), channel_id=1, source_target_pairs={{0,32},{32,0},{64,96},{96,64},{128,160},{160,128},{192,224},{224,1... | collective-permute-start | bytes 786440 | tf_op jit(solution)/shard_map/ppermute | solution.py:88
  171.1 10.6 %collective-permute-start.4 = (f32[256,256]{1,0:T(8,128)S(1)}, f32[256,256]{1,0:T(8,128)S(1)}, u32[]{:S(2)}, u32[]{:S(2)}) collective-permute-start(f32[256,256]{1,0:T(8,128)S(1)} %add.50), channel_id=1, source_target_pairs={{0,64},{32,96},{64,0},{96,32},{128,192},{160,224},{192,128},{224,1... | collective-permute-start | bytes 786440 | tf_op jit(solution)/shard_map/ppermute | solution.py:88
  181.7 17.4 %collective-permute-start.5 = (f32[256,256]{1,0:T(8,128)S(1)}, f32[256,256]{1,0:T(8,128)S(1)}, u32[]{:S(2)}, u32[]{:S(2)}) collective-permute-start(f32[256,256]{1,0:T(8,128)S(1)} %add.51), channel_id=1, source_target_pairs={{0,128},{32,160},{64,192},{96,224},{128,0},{160,32},{192,64},{224,... | collective-permute-start | bytes 786440 | tf_op jit(solution)/shard_map/ppermute | solution.py:88
  233.1 2.2 copy-start.1
  240.3 71.5 %all-to-all-start.1 = ((bf16[8,256,256]{2,1,0:T(8,128)(2,1)}), bf16[8,256,256]{2,1,0:T(8,128)(2,1)S(1)}, u32[]{:S(2)}, u32[]{:S(2)}) async-start(bf16[8,256,256]{2,1,0:T(8,128)(2,1)} %bitcast.5), calls=%async_computation.1 | async-start | bytes 2097152 | tf_op jit(solution)/shard_map/all_to_all | solution.py:78
  253.2 1.5 collective-permute-start.6
  254.8 24.4 %collective-permute-start.7 = (f32[256,256]{1,0:T(8,128)S(1)}, f32[256,256]{1,0:T(8,128)S(1)}, u32[]{:S(2)}, u32[]{:S(2)}) collective-permute-start(f32[256,256]{1,0:T(8,128)S(1)} %add.53), channel_id=1, source_target_pairs={{0,2},{1,3},{2,0},{3,1},{4,6},{5,7},{6,4},{7,5},{8,10},{9,11},{10,... | collective-permute-start | bytes 786440 | tf_op jit(solution)/shard_map/ppermute | solution.py:88
  279.2 14.5 %collective-permute-start.8 = (f32[256,256]{1,0:T(8,128)S(1)}, f32[256,256]{1,0:T(8,128)S(1)}, u32[]{:S(2)}, u32[]{:S(2)}) collective-permute-start(f32[256,256]{1,0:T(8,128)S(1)} %add.54), channel_id=1, source_target_pairs={{0,4},{1,5},{2,6},{3,7},{4,0},{5,1},{6,2},{7,3},{8,12},{9,13},{10,... | collective-permute-start | bytes 786440 | tf_op jit(solution)/shard_map/ppermute | solution.py:88
  293.7 8.0 %collective-permute-start.9 = (f32[256,256]{1,0:T(8,128)S(1)}, f32[256,256]{1,0:T(8,128)S(1)}, u32[]{:S(2)}, u32[]{:S(2)}) collective-permute-start(f32[256,256]{1,0:T(8,128)S(1)} %add.55), channel_id=1, source_target_pairs={{0,8},{1,9},{2,10},{3,11},{4,12},{5,13},{6,14},{7,15},{8,0},{9,1},... | collective-permute-start | bytes 786440 | tf_op jit(solution)/shard_map/ppermute | solution.py:88
  301.7 9.3 %collective-permute-start.10 = (f32[256,256]{1,0:T(8,128)S(1)}, f32[256,256]{1,0:T(8,128)S(1)}, u32[]{:S(2)}, u32[]{:S(2)}) collective-permute-start(f32[256,256]{1,0:T(8,128)S(1)} %add.56), channel_id=1, source_target_pairs={{0,16},{1,17},{2,18},{3,19},{4,20},{5,21},{6,22},{7,23},{8,24},{9,... | collective-permute-start | bytes 786440 | tf_op jit(solution)/shard_map/ppermute | solution.py:88
Sparse Core Ops, SparseCore 0:
  159.5 73.5 all-gather.1

commit v6 on v5

--- a/solution.py
+++ b/solution.py
@@ -3,6 +3,7 @@
 from jax import lax
 from jax.experimental import pallas as pl
 from jax.experimental.pallas import tpu as pltpu
+from jax.sharding import Mesh
 from jax.sharding import PartitionSpec as P
 
 GROUP = 64
@@ -104,6 +105,18 @@
     return value
 
 
+def reduce_pairs_then_blocks(partial_value, outer, inner):
+    outer_size = lax.axis_size(outer)
+    inner_size = lax.axis_size(inner)
+    pieces = partial_value.reshape(outer_size, inner_size, -1, partial_value.shape[1])
+    me = lax.axis_index(inner)
+    keep = jnp.take(pieces, me, axis=1)
+    send = jnp.take(pieces, inner_size - 1 - me, axis=1)
+    paired = keep + lax.ppermute(send, inner, [(i, inner_size - 1 - i) for i in range(inner_size)])
+    received = lax.all_to_all(paired.astype(jnp.bfloat16), outer, 0, 0, tiled=False)
+    return received.astype(jnp.float32).sum(0)
+
+
 def silu_grad(cot_part, pre_part):
     sigma = jax.nn.sigmoid(pre_part)
     return (cot_part.astype(jnp.float32) * (sigma * (1.0 + pre_part * (1.0 - sigma)))).astype(
@@ -114,7 +127,8 @@
 def per_device(features, weight, cotangent, tile_values, tile_rows, tile_cols, tile_count):
     node_rows = features.shape[0]
     row_devices = lax.axis_size("row")
-    col_devices = lax.axis_size("col")
+    col_axes = ("colhi", "core")
+    col_devices = lax.axis_size(col_axes)
     tile_block = tile_values[0]
     row_ids = tile_rows[0]
     col_ids = tile_cols[0]
@@ -122,9 +136,9 @@
     column_source = gather_pairs(features, "row")
     partial_value = tile_product(
         tile_block, row_ids, col_ids, occupied, column_source, col_devices * node_rows, False,
-        jnp.bfloat16,
+        jnp.float32,
     )
-    mixed = reduce_blocks(partial_value, "col", col_devices)
+    mixed = reduce_pairs_then_blocks(partial_value, "colhi", "core")
     pre = jnp.dot(
         mixed, weight.astype(jnp.float32), precision=lax.Precision.HIGHEST,
         preferred_element_type=jnp.float32,
@@ -136,14 +150,14 @@
     )
     grad_scale = float(node_rows * row_devices * col_devices) ** (-0.5)
     row_summed = butterfly_sum(local_term, ("row",))
-    row_source = lax.all_gather(grad_pre, "col", axis=0, tiled=True)
+    row_source = lax.all_gather(grad_pre, col_axes, axis=0, tiled=True)
     row_source, row_summed = lax.optimization_barrier((row_source, row_summed))
     output = jax.nn.silu(pre).astype(jnp.bfloat16)
     back_terms = tile_product(
         tile_block, row_ids, col_ids, occupied, row_source, row_devices * node_rows, True,
         jnp.bfloat16,
     )
-    weight_grad = butterfly_sum(row_summed, ("col",)) * grad_scale
+    weight_grad = butterfly_sum(row_summed, ("core", "colhi")) * grad_scale
     aggregated = reduce_blocks(back_terms, "row", row_devices)
     node_grad = aggregated.astype(jnp.bfloat16)
     feature_grad = jnp.dot(node_grad, weight.T, preferred_element_type=jnp.float32).astype(
@@ -153,19 +167,24 @@
 
 
 def solution(mesh):
+    cores = 2
+    devices = mesh.devices.reshape(mesh.shape["row"], mesh.shape["col"] // cores, cores)
+    split_mesh = Mesh(devices, ("row", "colhi", "core"))
+    nodes = ("row", "colhi", "core")
+    blocks = ("colhi", "core")
     placed = (
-        P(("row", "col"), None),
+        P(nodes, None),
         P(),
-        P(("row", "col"), None),
-        P("row", "col", None, None),
-        P("row", "col"),
-        P("row", "col"),
-        P("row", "col"),
+        P(nodes, None),
+        P("row", blocks, None, None),
+        P("row", blocks),
+        P("row", blocks),
+        P("row", blocks),
     )
     return jax.shard_map(
         per_device,
-        mesh=mesh,
+        mesh=split_mesh,
         in_specs=placed,
-        out_specs=(P(("row", "col"), None), P(("row", "col"), None), P()),
+        out_specs=(P(nodes, None), P(nodes, None), P()),
         check_vma=False,
     )

time: 324 us -> 295 us (0.910)
  blocking collectives: 110 us -> 65 us
  waiting for transfers between devices: 133 us -> 144 us
  other arithmetic: 3.1 us -> 11.4 us
  starting transfers between devices: 43.7 us -> 36.8 us
  Pallas kernels: 9.63 us -> 15.6 us
    all_to_all x1, blocking collectives: 110 us -> 65 us  [reduce_pairs_then_blocks(): lax.all_to_all(paired.astype(jnp.bfloat16), outer, 0, 0, tiled=False)]
    all_gather x1, waiting for transfers between devices: 34 us -> 44.6 us  [per_device(): row_source = lax.all_gather(grad_pre, col_axes, axis=0, tiled=True)]
    ppermute x0 -> x1, waiting for transfers between devices: none -> 7.5 us  [reduce_pairs_then_blocks(): lax.ppermute(send, inner, [(i, inner_size - 1 - i) for i in range(inner_s...]
    ppermute x8, waiting for transfers between devices: 77.5 us -> 70.8 us  [butterfly_sum(): value = value + lax.ppermute(value, axis, pairs)]
    pallas_call x2, Pallas kernels: 9.63 us -> 15.6 us  [tile_product(): pl.pallas_call(kernel, grid_spec=grid_spec, out_shape=jax.ShapeDtypeStruc...]
    all_to_all x1, starting transfers between devices: 12.9 us -> 8.37 us  [reduce_blocks(): received = lax.all_to_all(pieces, axis, 0, 0, tiled=False)]
    select_n x0 -> x1, other arithmetic: none -> 4.51 us  [reduce_pairs_then_blocks(): send = jnp.take(pieces, inner_size - 1 - me, axis=1)]
    convert_element_type x0 -> x1, other arithmetic: none -> 4.14 us  [reduce_pairs_then_blocks(): paired.astype(jnp.bfloat16)]
  transfers between devices with their start and end apart: 13 -> 14, of which waited for: 12 -> 13; matrix products, arithmetic and copies ran while one was open for 1% -> 1% of each run, Pallas kernels for 0% -> 0%
where the time goes in v6:
time: 295 us; the launch traced here: 293 us
  waiting for transfers between devices  144 us (49%)
  blocking collectives  65 us (22%)
  starting transfers between devices  36.8 us (12%)
  Pallas kernels  15.6 us (5%)
  between operations  14.8 us (5%)
  other arithmetic  11.4 us (4%)
  matrix products  3.23 us (1%)
    ppermute x8, waiting for transfers between devices, butterfly_sum(): value = value + lax.ppermute(value, axis, pairs)  70.8 us
    all_to_all x1, blocking collectives, reduce_pairs_then_blocks(): lax.all_to_all(paired.astype(jnp.bfloat16), outer, 0, 0, tiled=False)  65 us
    all_gather x1, waiting for transfers between devices, per_device(): row_source = lax.all_gather(grad_pre, col_axes, axis=0, tiled=True)  44.6 us
    ppermute x3, waiting for transfers between devices, gather_pairs(): other = lax.ppermute(value, axis, [(i, i ^ step) for i in range(size)])  21.2 us
    ppermute x8, starting transfers between devices, butterfly_sum(): value = value + lax.ppermute(value, axis, pairs)  16.2 us
    pallas_call x2, Pallas kernels, tile_product(): pl.pallas_call(kernel, grid_spec=grid_spec, out_shape=jax.ShapeDtypeStruc...  15.6 us
    ppermute x3, starting transfers between devices, gather_pairs(): other = lax.ppermute(value, axis, [(i, i ^ step) for i in range(size)])  12.2 us
    all_to_all x1, starting transfers between devices, reduce_blocks(): received = lax.all_to_all(pieces, axis, 0, 0, tiled=False)  8.37 us
  transfers between devices with their start and end apart: 14, of which 13 were waited for; matrix products, arithmetic and copies ran while one was open for 1% of the time, Pallas kernels for 0%

profile of v6, /device:TPU:4, one launch (start us, length us, event | category | flops | bytes accessed | tf_op | source)
XLA Modules:
  0.0 293.3 jit_solution(15732676695645002670)
XLA Ops:
  7.2 0.0 copy-start
  7.2 0.0 copy-start.2
  7.2 0.0 all-gather.2.cloned.1.call-start
  7.2 1.7 collective-permute-start
  8.9 3.9 %collective-permute-done = bf16[256,256]{1,0:T(8,128)(2,1)S(1)} collective-permute-done((bf16[256,256]{1,0:T(8,128)(2,1)}, bf16[256,256]{1,0:T(8,128)(2,1)S(1)}, u32[]{:S(2)}, u32[]{:S(2)}) %collective-permute-start) | collective-permute-done | bytes 131104 | tf_op jit(solution)/shard_map/ppermute | solution.py:99
  12.8 0.9 broadcast_select_fusion.5
  13.7 3.3 %collective-permute-start.1 = (bf16[512,256]{1,0:T(8,128)(2,1)S(1)}, bf16[512,256]{1,0:T(8,128)(2,1)S(1)}, u32[]{:S(2)}, u32[]{:S(2)}) collective-permute-start(bf16[512,256]{1,0:T(8,128)(2,1)S(1)} %pad_maximum_fusion.2), channel_id=1, source_target_pairs={{0,64},{32,96},{64,0},{96,32},{128,192},{160,224},{192,128},{224,1... | collective-permute-start | bytes 786440 | tf_op jit(solution)/shard_map/ppermute | solution.py:99
  17.0 5.5 %collective-permute-done.1 = bf16[512,256]{1,0:T(8,128)(2,1)S(1)} collective-permute-done((bf16[512,256]{1,0:T(8,128)(2,1)S(1)}, bf16[512,256]{1,0:T(8,128)(2,1)S(1)}, u32[]{:S(2)}, u32[]{:S(2)}) %collective-permute-start.1) | collective-permute-done | bytes 262176 | tf_op jit(solution)/shard_map/ppermute | solution.py:99
  22.5 0.1 broadcast_select_fusion.3
  22.7 7.3 %collective-permute-start.2 = (bf16[1024,256]{1,0:T(8,128)(2,1)S(1)}, bf16[1024,256]{1,0:T(8,128)(2,1)S(1)}, u32[]{:S(2)}, u32[]{:S(2)}) collective-permute-start(bf16[1024,256]{1,0:T(8,128)(2,1)S(1)} %pad_maximum_fusion.1), channel_id=1, source_target_pairs={{0,128},{32,160},{64,192},{96,224},{128,0},{160,32},{192,64},{224,... | collective-permute-start | bytes 1572872 | tf_op jit(solution)/shard_map/ppermute | solution.py:99
  30.6 11.8 %collective-permute-done.2 = bf16[1024,256]{1,0:T(8,128)(2,1)S(1)} collective-permute-done((bf16[1024,256]{1,0:T(8,128)(2,1)S(1)}, bf16[1024,256]{1,0:T(8,128)(2,1)S(1)}, u32[]{:S(2)}, u32[]{:S(2)}) %collective-permute-start.2) | collective-permute-done | bytes 524320 | tf_op jit(solution)/shard_map/ppermute | solution.py:99
  42.4 0.2 broadcast_select_fusion.1
  42.7 0.1 pad_maximum_fusion.src_ref
  42.7 9.3 %shard_map.94 = f32[8192,256]{1,0:T(8,128)} custom-call(s32[256]{0:T(256)S(1)} %bitcast.30, s32[256]{0:T(256)S(1)} %bitcast.32, s32[1]{0:T(128)} %bitcast.28.cnt_ref, bf16[256,128,128]{2,1,0:T(8,128)(2,1)} %bitcast.34, bf16[2048,256]{1,0:T(8,128)(2,1)S(1)} %pad_maximum_fusion.src_ref), custom_call_target="tpu_custom_call" | custom-call | tf_op jit(solution)/shard_map/pallas_call | solution.py:67
  52.1 4.5 %select_bitcast_fusion = f32[16,256,256]{2,1,0:T(8,128)} fusion(f32[16,2,256,256]{3,2,1,0:T(8,128)} %bitcast.36, s32[]{:T(128)S(6)} %select_n.87, pred[]{:T(512)S(6)} %and.38), kind=kLoop, calls=%fused_computation.4 | loop fusion | flops 1048576 | bytes 8388613 | tf_op jit(solution)/shard_map/jit(_take)/select_n | solution.py:114
  56.6 0.0 collective-permute-start.3
  56.6 7.5 %collective-permute-done.3 = f32[16,256,256]{2,1,0:T(8,128)} collective-permute-done((f32[16,256,256]{2,1,0:T(8,128)}, f32[16,256,256]{2,1,0:T(8,128)}, u32[]{:S(2)}, u32[]{:S(2)}) %collective-permute-start.3) | collective-permute-done | bytes 4194336 | tf_op jit(solution)/shard_map/ppermute | solution.py:115
  64.1 4.1 %fusion.2 = bf16[16,256,256]{2,1,0:T(8,128)(2,1)S(1)} fusion(f32[16,256,256]{2,1,0:T(8,128)} %collective-permute-done.3, f32[16,2,256,256]{3,2,1,0:T(8,128)} %bitcast.37, s32[]{:T(128)S(6)} %select_n.85, pred[]{:T(512)S(6)} %and.37), kind=kLoop, calls=%fused_computation.3 | loop fusion | flops 3145728 | bytes 10485765 | tf_op jit(solution)/shard_map/convert_element_type | solution.py:116
  68.2 0.0 copy-start.4
  68.3 65.0 %all_to_all.10 = bf16[16,256,256]{2,1,0:T(8,128)(2,1)S(1)} all-to-all(bf16[16,256,256]{2,1,0:T(8,128)(2,1)S(1)} %fusion.2), channel_id=1, replica_groups=mesh['row'=8,'colhi'=16,'core'=2] {'colhi'}, dimensions={0} | all-to-all | bytes 4194304 | tf_op jit(solution)/shard_map/all_to_all | solution.py:116
  133.2 0.3 convert_reduce_fusion
  133.5 1.1 multiply_convert_fusion
  134.6 0.0 all-gather.2.cloned.1.call-update
  134.6 1.3 fusion.3
  135.9 0.3 collective-permute-start.4
  136.2 6.9 %collective-permute-done.4 = f32[256,256]{1,0:T(8,128)S(1)} collective-permute-done((f32[256,256]{1,0:T(8,128)S(1)}, f32[256,256]{1,0:T(8,128)S(1)}, u32[]{:S(2)}, u32[]{:S(2)}) %collective-permute-start.4) | collective-permute-done | bytes 262176 | tf_op jit(solution)/shard_map/ppermute | solution.py:89
  143.1 2.5 collective-permute-start.5
  145.6 5.4 %collective-permute-done.5 = f32[256,256]{1,0:T(8,128)S(1)} collective-permute-done((f32[256,256]{1,0:T(8,128)S(1)}, f32[256,256]{1,0:T(8,128)S(1)}, u32[]{:S(2)}, u32[]{:S(2)}) %collective-permute-start.5) | collective-permute-done | bytes 262176 | tf_op jit(solution)/shard_map/ppermute | solution.py:89
  151.1 5.9 %collective-permute-start.6 = (f32[256,256]{1,0:T(8,128)S(1)}, f32[256,256]{1,0:T(8,128)S(1)}, u32[]{:S(2)}, u32[]{:S(2)}) collective-permute-start(f32[256,256]{1,0:T(8,128)S(1)} %add.58), channel_id=1, source_target_pairs={{0,128},{32,160},{64,192},{96,224},{128,0},{160,32},{192,64},{224,... | collective-permute-start | bytes 786440 | tf_op jit(solution)/shard_map/ppermute | solution.py:89
  157.0 4.7 %collective-permute-done.6 = f32[256,256]{1,0:T(8,128)S(1)} collective-permute-done((f32[256,256]{1,0:T(8,128)S(1)}, f32[256,256]{1,0:T(8,128)S(1)}, u32[]{:S(2)}, u32[]{:S(2)}) %collective-permute-start.6) | collective-permute-done | bytes 262176 | tf_op jit(solution)/shard_map/ppermute | solution.py:89
  161.7 44.6 %all-gather.2.cloned.1.call-done.src_ref = bf16[8192,256]{1,0:T(8,128)(2,1)} async-done(((bf16[256,256]{1,0:T(8,128)(2,1)}), bf16[8192,256]{1,0:T(8,128)(2,1)}) %all-gather.2.cloned.1.call-update) | async-done | bytes 4194320 | tf_op jit(solution)/shard_map/all_gather | solution.py:153
  206.3 2.2 copy-done.1
  208.5 6.3 %shard_map.95 = bf16[2048,256]{1,0:T(8,128)(2,1)} custom-call(s32[256]{0:T(256)S(1)} %bitcast.31, s32[256]{0:T(256)S(1)} %bitcast.33, s32[1]{0:T(128)} %bitcast.29.cnt_ref, bf16[256,128,128]{2,1,0:T(8,128)(2,1)} %bitcast.35, bf16[8192,256]{1,0:T(8,128)(2,1)S(1)} %copy-done.1), custom_call_target="tpu_custom_call" | custom-call | tf_op jit(solution)/shard_map/pallas_call | solution.py:67
  214.8 8.4 %all-to-all-start.1 = ((bf16[8,256,256]{2,1,0:T(8,128)(2,1)}), bf16[8,256,256]{2,1,0:T(8,128)(2,1)S(1)}, u32[]{:S(2)}, u32[]{:S(2)}) async-start(bf16[8,256,256]{2,1,0:T(8,128)(2,1)} %bitcast.7), calls=%async_computation.1 | async-start | bytes 2097152 | tf_op jit(solution)/shard_map/all_to_all | solution.py:79
  223.2 0.0 collective-permute-start.7
  223.2 1.5 collective-permute-done.7
  224.8 2.0 collective-permute-start.8
  226.7 27.4 %collective-permute-done.8 = f32[256,256]{1,0:T(8,128)S(1)} collective-permute-done((f32[256,256]{1,0:T(8,128)S(1)}, f32[256,256]{1,0:T(8,128)S(1)}, u32[]{:S(2)}, u32[]{:S(2)}) %collective-permute-start.8) | collective-permute-done | bytes 262176 | tf_op jit(solution)/shard_map/ppermute | solution.py:89
  254.2 1.7 collective-permute-start.9
  255.9 11.4 %collective-permute-done.9 = f32[256,256]{1,0:T(8,128)S(1)} collective-permute-done((f32[256,256]{1,0:T(8,128)S(1)}, f32[256,256]{1,0:T(8,128)S(1)}, u32[]{:S(2)}, u32[]{:S(2)}) %collective-permute-start.9) | collective-permute-done | bytes 262176 | tf_op jit(solution)/shard_map/ppermute | solution.py:89
  267.4 1.5 collective-permute-start.10
  268.9 6.8 %collective-permute-done.10 = f32[256,256]{1,0:T(8,128)S(1)} collective-permute-done((f32[256,256]{1,0:T(8,128)S(1)}, f32[256,256]{1,0:T(8,128)S(1)}, u32[]{:S(2)}, u32[]{:S(2)}) %collective-permute-start.10) | collective-permute-done | bytes 262176 | tf_op jit(solution)/shard_map/ppermute | solution.py:89
  275.7 2.3 collective-permute-start.11
  278.1 6.6 %collective-permute-done.11 = f32[256,256]{1,0:T(8,128)S(1)} collective-permute-done((f32[256,256]{1,0:T(8,128)S(1)}, f32[256,256]{1,0:T(8,128)S(1)}, u32[]{:S(2)}, u32[]{:S(2)}) %collective-permute-start.11) | collective-permute-done | bytes 262176 | tf_op jit(solution)/shard_map/ppermute | solution.py:89
  284.7 0.7 add_multiply_fusion
  285.4 0.0 all-to-all-done.1
  285.4 0.1 reduce_sum.22
  285.6 0.9 convolution_convert_fusion
  (15 shorter events, 0.3 us)
Async XLA Ops:
  7.2 126.4 %copy-start = (bf16[256,256]{1,0:T(8,128)(2,1)S(1)}, bf16[256,256]{1,0:T(8,128)(2,1)}, u32[]{:S(2)}) copy-start(bf16[256,256]{1,0:T(8,128)(2,1)} %param.10) | copy-start | bytes 393220
  7.2 35.6 %copy-start.2 = (s32[1,256]{1,0:T(1,128)S(1)}, s32[1,256]{1,0:T(1,128)}, u32[]{:S(2)}) copy-start(s32[1,256]{1,0:T(1,128)} %param.13) | copy-start | bytes 3076
  7.2 35.6 %copy-start.3 = (s32[1,256]{1,0:T(1,128)S(1)}, s32[1,256]{1,0:T(1,128)}, u32[]{:S(2)}) copy-start(s32[1,256]{1,0:T(1,128)} %param.14) | copy-start | bytes 3076
  7.2 199.1 %all-gather.2.cloned.1.call-start = ((), (), s32[]{:S(2)}) async-start(), calls=%async_computation.2 | async-start | bytes 4325376 | tf_op jit(solution)/shard_map/all_gather | solution.py:153
  7.2 5.5 %collective-permute-start = (bf16[256,256]{1,0:T(8,128)(2,1)}, bf16[256,256]{1,0:T(8,128)(2,1)S(1)}, u32[]{:S(2)}, u32[]{:S(2)}) collective-permute-start(bf16[256,256]{1,0:T(8,128)(2,1)} %param.9), channel_id=1, source_target_pairs={{0,32},{32,0},{64,96},{96,64},{128,160},{160,128},{192,224},{224,1... | collective-permute-start | bytes 393224 | tf_op jit(solution)/shard_map/ppermute | solution.py:99
  13.7 8.8 %collective-permute-start.1 = (bf16[512,256]{1,0:T(8,128)(2,1)S(1)}, bf16[512,256]{1,0:T(8,128)(2,1)S(1)}, u32[]{:S(2)}, u32[]{:S(2)}) collective-permute-start(bf16[512,256]{1,0:T(8,128)(2,1)S(1)} %pad_maximum_fusion.2), channel_id=1, source_target_pairs={{0,64},{32,96},{64,0},{96,32},{128,192},{160,224},{192,128},{224,1... | collective-permute-start | bytes 786440 | tf_op jit(solution)/shard_map/ppermute | solution.py:99
  22.7 19.8 %collective-permute-start.2 = (bf16[1024,256]{1,0:T(8,128)(2,1)S(1)}, bf16[1024,256]{1,0:T(8,128)(2,1)S(1)}, u32[]{:S(2)}, u32[]{:S(2)}) collective-permute-start(bf16[1024,256]{1,0:T(8,128)(2,1)S(1)} %pad_maximum_fusion.1), channel_id=1, source_target_pairs={{0,128},{32,160},{64,192},{96,224},{128,0},{160,32},{192,64},{224,... | collective-permute-start | bytes 1572872 | tf_op jit(solution)/shard_map/ppermute | solution.py:99
  56.6 7.5 %collective-permute-start.3 = (f32[16,256,256]{2,1,0:T(8,128)}, f32[16,256,256]{2,1,0:T(8,128)}, u32[]{:S(2)}, u32[]{:S(2)}) collective-permute-start(f32[16,256,256]{2,1,0:T(8,128)} %select_bitcast_fusion), channel_id=1, source_target_pairs={{0,1},{1,0},{2,3},{3,2},{4,5},{5,4},{6,7},{7,6},{8,9},{9,8},{10,11... | collective-permute-start | bytes 12582920 | tf_op jit(solution)/shard_map/ppermute | solution.py:115
  68.2 65.3 %copy-start.4 = (bf16[256,256]{1,0:T(8,128)(2,1)S(1)}, bf16[256,256]{1,0:T(8,128)(2,1)}, u32[]{:S(2)}) copy-start(bf16[256,256]{1,0:T(8,128)(2,1)} %param.11) | copy-start | bytes 393220
  135.9 7.1 %collective-permute-start.4 = (f32[256,256]{1,0:T(8,128)S(1)}, f32[256,256]{1,0:T(8,128)S(1)}, u32[]{:S(2)}, u32[]{:S(2)}) collective-permute-start(f32[256,256]{1,0:T(8,128)S(1)} %fusion.3), channel_id=1, source_target_pairs={{0,32},{32,0},{64,96},{96,64},{128,160},{160,128},{192,224},{224,1... | collective-permute-start | bytes 786440 | tf_op jit(solution)/shard_map/ppermute | solution.py:89
  143.1 8.0 %collective-permute-start.5 = (f32[256,256]{1,0:T(8,128)S(1)}, f32[256,256]{1,0:T(8,128)S(1)}, u32[]{:S(2)}, u32[]{:S(2)}) collective-permute-start(f32[256,256]{1,0:T(8,128)S(1)} %add.57), channel_id=1, source_target_pairs={{0,64},{32,96},{64,0},{96,32},{128,192},{160,224},{192,128},{224,1... | collective-permute-start | bytes 786440 | tf_op jit(solution)/shard_map/ppermute | solution.py:89
  151.1 10.6 %collective-permute-start.6 = (f32[256,256]{1,0:T(8,128)S(1)}, f32[256,256]{1,0:T(8,128)S(1)}, u32[]{:S(2)}, u32[]{:S(2)}) collective-permute-start(f32[256,256]{1,0:T(8,128)S(1)} %add.58), channel_id=1, source_target_pairs={{0,128},{32,160},{64,192},{96,224},{128,0},{160,32},{192,64},{224,... | collective-permute-start | bytes 786440 | tf_op jit(solution)/shard_map/ppermute | solution.py:89
  206.3 2.2 copy-start.1
  214.8 70.6 %all-to-all-start.1 = ((bf16[8,256,256]{2,1,0:T(8,128)(2,1)}), bf16[8,256,256]{2,1,0:T(8,128)(2,1)S(1)}, u32[]{:S(2)}, u32[]{:S(2)}) async-start(bf16[8,256,256]{2,1,0:T(8,128)(2,1)} %bitcast.7), calls=%async_computation.1 | async-start | bytes 2097152 | tf_op jit(solution)/shard_map/all_to_all | solution.py:79
  223.2 1.5 collective-permute-start.7
  224.8 29.4 %collective-permute-start.8 = (f32[256,256]{1,0:T(8,128)S(1)}, f32[256,256]{1,0:T(8,128)S(1)}, u32[]{:S(2)}, u32[]{:S(2)}) collective-permute-start(f32[256,256]{1,0:T(8,128)S(1)} %add.60), channel_id=1, source_target_pairs={{0,2},{2,0},{4,6},{6,4},{8,10},{10,8},{12,14},{14,12},{16,18},{18,... | collective-permute-start | bytes 786440 | tf_op jit(solution)/shard_map/ppermute | solution.py:89
  254.2 13.2 %collective-permute-start.9 = (f32[256,256]{1,0:T(8,128)S(1)}, f32[256,256]{1,0:T(8,128)S(1)}, u32[]{:S(2)}, u32[]{:S(2)}) collective-permute-start(f32[256,256]{1,0:T(8,128)S(1)} %add.61), channel_id=1, source_target_pairs={{0,4},{2,6},{4,0},{6,2},{8,12},{10,14},{12,8},{14,10},{16,20},{18,... | collective-permute-start | bytes 786440 | tf_op jit(solution)/shard_map/ppermute | solution.py:89
  267.4 8.3 %collective-permute-start.10 = (f32[256,256]{1,0:T(8,128)S(1)}, f32[256,256]{1,0:T(8,128)S(1)}, u32[]{:S(2)}, u32[]{:S(2)}) collective-permute-start(f32[256,256]{1,0:T(8,128)S(1)} %add.62), channel_id=1, source_target_pairs={{0,8},{2,10},{4,12},{6,14},{8,0},{10,2},{12,4},{14,6},{16,24},{18,... | collective-permute-start | bytes 786440 | tf_op jit(solution)/shard_map/ppermute | solution.py:89
  275.7 9.0 %collective-permute-start.11 = (f32[256,256]{1,0:T(8,128)S(1)}, f32[256,256]{1,0:T(8,128)S(1)}, u32[]{:S(2)}, u32[]{:S(2)}) collective-permute-start(f32[256,256]{1,0:T(8,128)S(1)} %add.63), channel_id=1, source_target_pairs={{0,16},{2,18},{4,20},{6,22},{8,24},{10,26},{12,28},{14,30},{16,0},... | collective-permute-start | bytes 786440 | tf_op jit(solution)/shard_map/ppermute | solution.py:89
Sparse Core Ops, SparseCore 0:
  134.7 71.5 all-gather.1
